TPU v7x, 256 devices: a whole 4x4x8 slice. The times are simulated.
256 devices in a mesh: batch: 8 (over x, core), tensor: 32 (over y, z).
Axes of the slice: x: 4, y: 4, z: 8, core: 2. Of those that a mesh axis runs over, the one named last changes fastest.
Arguments:
- inputs: bfloat16 [4, 8, 32, 4096], P(None, 'batch', 'tensor'), may hold values from -6 to 6
- norm_gain: float32 [4096], replicated, may hold values from 0.5 to 1.5
- norm_bias: float32 [4096], replicated, may hold values from -3 to 3
- qkv_weight: bfloat16 [4096, 3, 4096], P(None, None, 'tensor'), may hold values from -0.09375 to 0.09375
- out_weight: bfloat16 [4096, 4096], P('tensor'), may hold values from -0.375 to 0.375
- in_weight: bfloat16 [4096, 8192], P(None, 'tensor'), may hold values from -0.09375 to 0.09375
- in_bias: float32 [8192], P('tensor'), may hold values from -3 to 3
- down_weight: bfloat16 [8192, 4096], P('tensor'), may hold values from -0.0625 to 0.0625
- down_bias: float32 [4096], replicated, may hold values from -3 to 3
- page_pool: bfloat16 [128, 2, 128, 4096], P('batch', None, None, 'tensor'), may hold values from -103 to 103
- old_cache: bfloat16 [8, 32, 2, 64, 4096], P('batch', None, None, None, 'tensor'), may hold values from -103 to 103, as said below
- page_table: int32 [32, 4], replicated, may hold values from 0 to 127, as said below
- prompt_length: int32 [32], replicated, may hold values from 1 to 512, 8192 in all
- parents: int32 [4, 8, 32], replicated, may hold values from 0 to 7
Outputs:
- outputs: float32 [4, 8, 32, 4096], P(None, 'batch', 'tensor')
Inputs may be any that keep to these rules, and one draw needn't show every extreme that they name: `old_cache`: key and value entries of the beams' generated tokens. `page_table`: every pool page is named exactly once in the table. The pool is cut into as many equal blocks of consecutive pages as the batch axis has devices; request r names only pages of block r modulo that count.
All inputs are finite; a program needn't handle non-finite values.
Results may differ from a plain program's by a relative error of at most 0.034.
Values may be sent and summed in bfloat16 or wider, within the bound.
No kernel may reach another device: no remote copies, remote signals or barrier semaphores. Data moves between devices by JAX's collectives and lax.ppermute only.
A program may use at most 128 MiB of HBM per device.

v0:
```python
import math

import jax
import jax.numpy as jnp
from jax import lax
from jax.sharding import PartitionSpec as P

HDIM = 256
ROT = 64
BEAMS = 8
STEPS = 4


NEG_FILL = -1e30


def partner(value, axis, bit):
    return lax.ppermute(value, axis, [(i, i ^ 1 << bit) for i in range(lax.axis_size(axis))])


def joined_2(part, axis, combine):
    gathered = jax.tree.map(lambda a: lax.all_gather(a, axis), part)

    def take(source):
        return jax.tree.map(lambda a: lax.dynamic_index_in_dim(a, source, 0, False), gathered)

    return lax.fori_loop(
        1, lax.axis_size(axis), lambda source, state: combine(state, take(source)), take(0)
    )


def normalize(row_block, norm_gain, norm_bias):
    widened = row_block.astype(jnp.float32)
    center = jnp.mean(widened, axis=-1, keepdims=True)
    shifted = widened - center
    variance = jnp.mean(shifted * shifted, axis=-1, keepdims=True)
    return shifted * lax.rsqrt(variance + 1e-05) * norm_gain + norm_bias


def rotate_local(vectors, position, first_column):
    half_count = vectors.shape[-1] // 2
    doubled = (first_column + 2 * jnp.arange(half_count)) % HDIM
    exponent = doubled.astype(jnp.float32) / ROT
    frequency = jnp.where(doubled < ROT, jnp.exp(-exponent * math.log(10000.0)), 0.0)
    angles = position[:, None] * frequency[None, :]
    cosine = jnp.cos(angles)[None]
    sine_part = jnp.sin(angles)[None]
    halves = vectors.reshape(vectors.shape[:-1] + (half_count, 2))
    even_part = halves[..., 0]
    odd_part = halves[..., 1]
    turned = jnp.stack(
        [even_part * cosine - odd_part * sine_part, odd_part * cosine + even_part * sine_part],
        axis=-1,
    )
    return turned.reshape(vectors.shape)


def combine(earlier, later):
    peak_one, total_one, mixture_one = earlier
    peak_two, total_two, mixture_two = later
    peak = jnp.maximum(peak_one, peak_two)
    factor_one = jnp.exp(peak_one - peak)
    factor_two = jnp.exp(peak_two - peak)
    return (
        peak,
        total_one * factor_one + total_two * factor_two,
        mixture_one * factor_one[..., None] + mixture_two * factor_two[..., None],
    )


def partial_softmax(scores, allowed):
    masked = jnp.where(allowed, scores, NEG_FILL)
    peak = jnp.max(masked, axis=-1)
    weights = jnp.where(allowed, jnp.exp(masked - peak[..., None]), 0.0)
    return (peak, jnp.sum(weights, axis=-1), weights.astype(jnp.bfloat16))


def place_block(values, slot, slot_count, axis, fill_value):
    hit_shape = [1] * (values.ndim + 1)
    hit_shape[axis] = slot_count
    hits = (jnp.arange(slot_count) == slot).reshape(hit_shape)
    return jnp.where(hits, jnp.expand_dims(values, axis), fill_value)


def head_sum(prompt_scores, chain_scores):
    other_prompt, other_chain = partner((prompt_scores, chain_scores), "tensor", 0)
    prompt_scores = prompt_scores + other_prompt
    chain_scores = chain_scores + other_chain
    return (prompt_scores, chain_scores)


def on_device(
    inputs,
    norm_gain,
    norm_bias,
    qkv_weight,
    out_weight,
    in_weight,
    in_bias,
    down_weight,
    down_bias,
    page_pool,
    old_cache,
    page_table,
    prompt_length,
    parents,
):
    batch_index = lax.axis_index("batch")
    tensor_index = lax.axis_index("tensor")
    groups = lax.axis_size("batch")
    beam_dev = inputs.shape[1]
    model_width = inputs.shape[3]
    columns = qkv_weight.shape[2]
    requests = page_table.shape[0]
    history = old_cache.shape[3]
    prompt_span = page_table.shape[1] * page_pool.shape[2]
    heads_dev = max(columns // HDIM, 1)
    head_part = min(columns, HDIM)
    scale_factor = HDIM ** (-0.5)
    qkv_flat = qkv_weight.reshape(model_width, 3 * columns)
    first_column = tensor_index * columns
    owners = batch_index * beam_dev + jnp.arange(beam_dev)
    old_keys = old_cache[:, :, 0].reshape(beam_dev, requests, history, heads_dev, head_part)
    old_values = old_cache[:, :, 1].reshape(beam_dev, requests, history, heads_dev, head_part)
    stored_keys = jnp.zeros((beam_dev, requests, STEPS, columns), jnp.bfloat16)
    stored_values = jnp.zeros((beam_dev, requests, STEPS, columns), jnp.bfloat16)
    beam_ids = jnp.broadcast_to(jnp.arange(BEAMS)[:, None], (BEAMS, requests))
    prompt_ok = jnp.arange(prompt_span)[None, :] < prompt_length[:, None]
    whole_pool = lax.all_gather(page_pool, "batch", axis=0, tiled=True)
    page_rows = whole_pool[page_table]
    count_rows = page_table.shape[0]
    prompt_keys = page_rows[:, :, 0].reshape(count_rows, prompt_span, heads_dev, head_part)
    prompt_values = page_rows[:, :, 1].reshape(count_rows, prompt_span, heads_dev, head_part)
    outputs = []
    for step_index in range(STEPS):
        current = inputs[step_index]
        normed = normalize(current, norm_gain, norm_bias).astype(jnp.bfloat16)
        gathered_rows = lax.all_gather(normed, "tensor", axis=1, tiled=True)
        attn_part = jnp.einsum(
            "brd,dc->brc", gathered_rows, qkv_flat, preferred_element_type=jnp.float32
        )
        ffn_part = jnp.einsum(
            "brd,dc->brc", gathered_rows, in_weight, preferred_element_type=jnp.float32
        )
        projected = jnp.concatenate([attn_part, ffn_part], axis=-1)
        position = (prompt_length + history + step_index).astype(jnp.float32)
        queries = rotate_local(projected[..., :columns], position, first_column).astype(
            jnp.bfloat16
        )
        fresh_keys = rotate_local(
            projected[..., columns : 2 * columns], position, first_column
        ).astype(jnp.bfloat16)
        fresh_values = projected[..., 2 * columns : 3 * columns].astype(jnp.bfloat16)
        hidden = jax.nn.gelu(projected[..., 3 * columns :] + in_bias, approximate=True).astype(
            jnp.bfloat16
        )
        stored_keys = stored_keys.at[:, :, step_index].set(fresh_keys)
        stored_values = stored_values.at[:, :, step_index].set(fresh_values)
        queries_all = lax.all_gather(queries, "batch", axis=0, tiled=True)
        query_heads = queries_all.reshape(BEAMS, requests, heads_dev, head_part)
        own_heads = queries.reshape(beam_dev, requests, heads_dev, head_part)
        ancestry = []
        lineage = beam_ids
        for back_step in range(step_index, -1, -1):
            ancestry.append(lineage)
            lineage = jnp.take_along_axis(parents[back_step], lineage, axis=0)
        unused_steps = [jnp.full_like(beam_ids, -1)] * (STEPS - 1 - step_index)
        ancestry_all = jnp.stack(ancestry[::-1] + unused_steps, axis=-1)
        stored_k = stored_keys.reshape(beam_dev, requests, STEPS, heads_dev, head_part)
        stored_v = stored_values.reshape(beam_dev, requests, STEPS, heads_dev, head_part)
        chain_scores = (
            jnp.concatenate(
                [
                    jnp.einsum(
                        "brnd,jrtnd->brnjt",
                        query_heads,
                        old_keys,
                        preferred_element_type=jnp.float32,
                    ),
                    jnp.einsum(
                        "brnd,jrtnd->brnjt",
                        query_heads,
                        stored_k,
                        preferred_element_type=jnp.float32,
                    ),
                ],
                axis=-1,
            )
            * scale_factor
        )
        old_ok = jnp.broadcast_to(
            (lineage[:, :, None] == owners[None, None, :])[:, :, :, None],
            (BEAMS, requests, beam_dev, history),
        )
        new_ok = ancestry_all[:, :, None, :] == owners[None, None, :, None]
        chain_ok = jnp.concatenate([old_ok, new_ok], axis=-1)
        prompt_scores = (
            jnp.einsum(
                "brnd,rtnd->brnt", own_heads, prompt_keys, preferred_element_type=jnp.float32
            )
            * scale_factor
        )
        prompt_scores, chain_scores = head_sum(prompt_scores, chain_scores)
        prompt_peak, prompt_total, prompt_weights = partial_softmax(
            prompt_scores, prompt_ok[None, :, None, :]
        )
        prompt_mix = jnp.einsum(
            "brnt,rtnd->brnd", prompt_weights, prompt_values, preferred_element_type=jnp.float32
        )
        peak_full = place_block(prompt_peak, batch_index, groups, 0, NEG_FILL).reshape(
            BEAMS, requests, heads_dev
        )
        total_full = place_block(prompt_total, batch_index, groups, 0, 0.0).reshape(
            BEAMS, requests, heads_dev
        )
        mix_full = place_block(prompt_mix, batch_index, groups, 0, 0.0).reshape(
            BEAMS, requests, heads_dev, head_part
        )
        chain_peak, chain_total, chain_weights = partial_softmax(
            chain_scores.reshape(BEAMS, requests, heads_dev, -1), chain_ok
        )
        chain_weights = chain_weights.reshape(BEAMS, requests, heads_dev, beam_dev, history + STEPS)
        chain_mix = jnp.einsum(
            "brnjt,jrtnd->brnd",
            chain_weights[..., :history],
            old_values,
            preferred_element_type=jnp.float32,
        )
        chain_mix = chain_mix + jnp.einsum(
            "brnjt,jrtnd->brnd",
            chain_weights[..., history:],
            stored_v,
            preferred_element_type=jnp.float32,
        )
        joined = combine((peak_full, total_full, mix_full), (chain_peak, chain_total, chain_mix))
        merged = joined_2((joined[0], joined[1], joined[2]), "batch", combine)
        first_beam = batch_index * beam_dev
        total_own = lax.dynamic_slice_in_dim(merged[1], first_beam, beam_dev, 0)
        mix_own = lax.dynamic_slice_in_dim(merged[2], first_beam, beam_dev, 0)
        attention = (
            (mix_own / total_own[..., None])
            .reshape(beam_dev, requests, columns)
            .astype(jnp.bfloat16)
        )
        summed = lax.psum_scatter(
            jnp.einsum("brc,cd->rbd", attention, out_weight, preferred_element_type=jnp.float32)
            + jnp.einsum("brf,fd->rbd", hidden, down_weight, preferred_element_type=jnp.float32),
            "tensor",
            scatter_dimension=0,
            tiled=True,
        )
        update = jnp.transpose(summed, (1, 0, 2))
        result = current.astype(jnp.float32) + update + down_bias
        outputs.append(result)
    return jnp.stack(outputs, axis=0)


def solution(mesh):
    in_specs = (
        P(None, "batch", "tensor", None),
        P(),
        P(),
        P(None, None, "tensor"),
        P("tensor", None),
        P(None, "tensor"),
        P("tensor"),
        P("tensor", None),
        P(),
        P("batch", None, None, "tensor"),
        P("batch", None, None, None, "tensor"),
        P(),
        P(),
        P(),
    )
    out_specs = P(None, "batch", "tensor", None)
    return jax.shard_map(
        on_device, mesh=mesh, in_specs=in_specs, out_specs=out_specs, check_vma=False
    )
```

profile of v0, /device:TPU:2, one launch (start us, length us, event | category | flops | bytes accessed | tf_op | source)
XLA Modules:
  0.0 820.2 jit_solution(18254087234877689215)
XLA Ops:
  17.8 52.7 %all-gather.4 = bf16[131072]{0:T(1024)(128)(2,1)S(1)} all-gather(bf16[4096]{0:T(1024)(128)(2,1)S(1)} %get-tuple-element.1398), channel_id=6, replica_groups=mesh['batch'=8,'tensor'=32] {'tensor'}, dimensions={0}, use_global_device_ids=true | all-gather | bytes 270336 | tf_op jit(solution)/shard_map/all_gather | solution.py:138
  70.6 48.3 %all-gather.2 = bf16[131072]{0:T(1024)(128)(2,1)S(1)} all-gather(bf16[4096]{0:T(1024)(128)(2,1)S(1)} %get-tuple-element.1399), channel_id=4, replica_groups=mesh['batch'=8,'tensor'=32] {'tensor'}, dimensions={0}, use_global_device_ids=true | all-gather | bytes 270336 | tf_op jit(solution)/shard_map/all_gather | solution.py:138
  119.0 47.0 %all-gather = bf16[131072]{0:T(1024)(128)(2,1)S(1)} all-gather(bf16[4096]{0:T(1024)(128)(2,1)S(1)} %get-tuple-element.1400), channel_id=2, replica_groups=mesh['batch'=8,'tensor'=32] {'tensor'}, dimensions={0}, use_global_device_ids=true | all-gather | bytes 270336 | tf_op jit(solution)/shard_map/all_gather | solution.py:138
  166.8 48.2 %all-gather.6 = bf16[131072]{0:T(1024)(128)(2,1)S(1)} all-gather(bf16[4096]{0:T(1024)(128)(2,1)S(1)} %get-tuple-element.1401), channel_id=8, replica_groups=mesh['batch'=8,'tensor'=32] {'tensor'}, dimensions={0}, use_global_device_ids=true | all-gather | bytes 270336 | tf_op jit(solution)/shard_map/all_gather | solution.py:138
  215.2 4.8 copy.1379
  220.0 2.9 convolution_bitcast_fusion.12
  224.5 2.9 convolution_bitcast_fusion.13
  229.5 2.9 convolution_bitcast_fusion.14
  234.6 3.1 convolution_bitcast_fusion.15
  278.8 12.8 %all_gather.91 = bf16[8,32,128]{2,1,0:T(8,128)(2,1)S(1)} all-gather(bf16[1,32,128]{2,1,0:T(8,128)(2,1)S(1)} %copy.1416), channel_id=1, replica_groups=mesh['batch'=8,'tensor'=32] {'batch'}, dimensions={0}, use_global_device_ids=true | all-gather | bytes 73728 | tf_op jit(solution)/shard_map/all_gather | solution.py:159
  293.2 13.0 %all_gather.97 = bf16[8,32,128]{2,1,0:T(8,128)(2,1)S(1)} all-gather(bf16[1,32,128]{2,1,0:T(8,128)(2,1)} %copy.1443), channel_id=1, replica_groups=mesh['batch'=8,'tensor'=32] {'batch'}, dimensions={0}, use_global_device_ids=true | all-gather | bytes 73728 | tf_op jit(solution)/shard_map/all_gather | solution.py:159
  307.7 13.1 %all_gather.103 = bf16[8,32,128]{2,1,0:T(8,128)(2,1)S(1)} all-gather(bf16[1,32,128]{2,1,0:T(8,128)(2,1)} %copy.1470), channel_id=1, replica_groups=mesh['batch'=8,'tensor'=32] {'batch'}, dimensions={0}, use_global_device_ids=true | all-gather | bytes 73728 | tf_op jit(solution)/shard_map/all_gather | solution.py:159
  325.5 2.0 collective-permute-start.5
  329.5 12.8 %all_gather.85 = bf16[8,32,128]{2,1,0:T(8,128)(2,1)S(1)} all-gather(bf16[1,32,128]{2,1,0:T(8,128)(2,1)S(1)} %copy.1387), channel_id=1, replica_groups=mesh['batch'=8,'tensor'=32] {'batch'}, dimensions={0}, use_global_device_ids=true | all-gather | bytes 73728 | tf_op jit(solution)/shard_map/all_gather | solution.py:159
  343.6 2.0 collective-permute-start.1
  396.3 10.0 %gather_fusion = bf16[128,2,128,128]{3,2,1,0:T(8,128)(2,1)} fusion(bf16[128,2,128,128]{3,2,1,0:T(8,128)(2,1)} %all-gather.14.cloned.1.call-done, s32[1024]{0:T(1024)S(1)} %pad_clamp_fusion), kind=kCustom, calls=%fused_computation.10 | custom fusion | bytes 16777728 | tf_op jit(solution)/shard_map/gather | solution.py:130
  406.3 4.0 fusion.287
  415.6 2.0 collective-permute-start.4
  417.7 1.9 collective-permute-start
  428.0 3.8 fusion.107
  431.8 3.8 fusion.80
  437.9 2.8 fusion.52
  446.8 2.8 fusion.48
  451.2 3.8 fusion.89
  455.0 3.7 fusion.98
  465.0 12.9 %all_gather.87 = f32[8,8,32,1]{2,1,3,0:T(8,128)S(1)} all-gather(f32[1,8,32,1]{2,1,3,0:T(8,128)S(1)} %get-tuple-element.1418), channel_id=1, replica_groups=mesh['batch'=8,'tensor'=32] {'batch'}, dimensions={0}, use_global_device_ids=true | all-gather | bytes 9216 | tf_op jit(solution)/shard_map/all_gather | solution.py:22
  477.9 12.9 %all_gather.86 = f32[8,8,32,1]{2,1,3,0:T(8,128)S(1)} all-gather(f32[1,8,32,1]{2,1,3,0:T(8,128)S(1)} %get-tuple-element.1419), channel_id=1, replica_groups=mesh['batch'=8,'tensor'=32] {'batch'}, dimensions={0}, use_global_device_ids=true | all-gather | bytes 9216 | tf_op jit(solution)/shard_map/all_gather | solution.py:22
  490.8 12.9 %all_gather.104 = f32[8,8,32,1]{2,1,3,0:T(8,128)S(1)} all-gather(f32[1,8,32,1]{2,1,3,0:T(8,128)S(1)} %get-tuple-element.1443), channel_id=1, replica_groups=mesh['batch'=8,'tensor'=32] {'batch'}, dimensions={0}, use_global_device_ids=true | all-gather | bytes 9216 | tf_op jit(solution)/shard_map/all_gather | solution.py:22
  503.7 13.1 %all_gather.105 = f32[8,8,32,1]{2,1,3,0:T(8,128)S(1)} all-gather(f32[1,8,32,1]{2,1,3,0:T(8,128)S(1)} %get-tuple-element.1444), channel_id=1, replica_groups=mesh['batch'=8,'tensor'=32] {'batch'}, dimensions={0}, use_global_device_ids=true | all-gather | bytes 9216 | tf_op jit(solution)/shard_map/all_gather | solution.py:22
  516.8 12.9 %all_gather.98 = f32[8,8,32,1]{2,1,3,0:T(8,128)S(1)} all-gather(f32[1,8,32,1]{2,1,3,0:T(8,128)S(1)} %get-tuple-element.1445), channel_id=1, replica_groups=mesh['batch'=8,'tensor'=32] {'batch'}, dimensions={0}, use_global_device_ids=true | all-gather | bytes 9216 | tf_op jit(solution)/shard_map/all_gather | solution.py:22
  529.6 12.9 %all_gather.99 = f32[8,8,32,1]{2,1,3,0:T(8,128)S(1)} all-gather(f32[1,8,32,1]{2,1,3,0:T(8,128)S(1)} %get-tuple-element.1446), channel_id=1, replica_groups=mesh['batch'=8,'tensor'=32] {'batch'}, dimensions={0}, use_global_device_ids=true | all-gather | bytes 9216 | tf_op jit(solution)/shard_map/all_gather | solution.py:22
  542.5 12.9 %all_gather.92 = f32[8,8,32,1]{2,1,3,0:T(8,128)S(1)} all-gather(f32[1,8,32,1]{2,1,3,0:T(8,128)S(1)} %get-tuple-element.1447), channel_id=1, replica_groups=mesh['batch'=8,'tensor'=32] {'batch'}, dimensions={0}, use_global_device_ids=true | all-gather | bytes 9216 | tf_op jit(solution)/shard_map/all_gather | solution.py:22
  555.3 12.9 %all_gather.93 = f32[8,8,32,1]{2,1,3,0:T(8,128)S(1)} all-gather(f32[1,8,32,1]{2,1,3,0:T(8,128)S(1)} %get-tuple-element.1448), channel_id=1, replica_groups=mesh['batch'=8,'tensor'=32] {'batch'}, dimensions={0}, use_global_device_ids=true | all-gather | bytes 9216 | tf_op jit(solution)/shard_map/all_gather | solution.py:22
  568.2 2.8 fusion.50
  573.9 16.4 %while.84 = (s32[]{:T(128)}, f32[8,32,1]{1,2,0:T(1,128)S(1)}, f32[8,32,1]{1,2,0:T(1,128)S(1)}, f32[8,32,1,128]{3,2,1,0:T(1,128)S(1)}, f32[8,8,32,1]{2,1,3,0:T(8,...) while((s32[]{:T(128)}, f32[8,32,1]{1,2,0:T(1,128)S(1)}, ...), condition=%wide.region_7.9_spmd, body=%wide.region_6.8_spmd.sunk | while | flops 99845 | bytes 931983 | solution.py:27
  591.4 11.7 %while.85 = (s32[]{:T(128)}, f32[8,32,1]{1,2,0:T(1,128)S(1)}, f32[8,32,1]{1,2,0:T(1,128)S(1)}, f32[8,32,1,128]{3,2,1,0:T(1,128)S(1)}, f32[8,8,32,1]{2,1,3,0:T(8,...) while((s32[]{:T(128)}, f32[8,32,1]{1,2,0:T(1,128)S(1)}, ...), condition=%wide.region_16.18_spmd, body=%wide.region_15.17_spmd.sunk | while | flops 99845 | bytes 931983 | solution.py:27
  604.3 16.4 %while.87 = (s32[]{:T(128)}, f32[8,32,1]{1,2,0:T(1,128)S(1)}, f32[8,32,1]{1,2,0:T(1,128)S(1)}, f32[8,32,1,128]{3,2,1,0:T(1,128)S(1)}, f32[8,8,32,1]{2,1,3,0:T(8,...) while((s32[]{:T(128)}, f32[8,32,1]{1,2,0:T(1,128)S(1)}, ...), condition=%wide.region_34.36_spmd, body=%wide.region_33.35_spmd.sunk | while | flops 99845 | bytes 931983 | solution.py:27
  624.2 26.7 %while.86 = (s32[]{:T(128)}, f32[8,32,1]{1,2,0:T(1,128)S(1)}, f32[8,32,1]{1,2,0:T(1,128)S(1)}, f32[8,32,1,128]{3,2,1,0:T(1,128)}, f32[8,8,32,1]{2,1,3,0:T(8,128)...) while((s32[]{:T(128)}, f32[8,32,1]{1,2,0:T(1,128)S(1)}, ...), condition=%wide.region_25.27_spmd, body=%wide.region_24.26_spmd.sunk | while | flops 99845 | bytes 931983 | solution.py:27
  625.9 2.2 multiply_add_fusion.21
  629.7 2.2 multiply_add_fusion.21
  633.5 2.2 multiply_add_fusion.21
  637.3 2.2 multiply_add_fusion.21
  641.1 2.2 multiply_add_fusion.21
  644.9 2.2 multiply_add_fusion.21
  648.8 2.2 multiply_add_fusion.21
  650.9 2.3 fusion
  653.2 2.2 fusion.1
  659.1 151.5 %all-reduce.9.cloned.1.call-done = (f32[32,1,4096]{2,0,1:T(8,128)}, f32[32,1,4096]{2,0,1:T(8,128)}, f32[32,1,4096]{2,0,1:T(8,128)}, f32[32,1,4096]{2,0,1:T(8,128)}) async-done(((f32[32,1,4096]{2,0,1:T(8,128)}, f32[32,1,4096]{2,0,1:T(8,128)}, f32[32,1,4096]{2,0,1:T(8,128)}, f32[32,1,4096]{2,0,1:T(8,128)}), (f32[32,1,4096]{2,0,1:T(8,128)}, f32[32,1,4096]{2,0,1:T(8,128)}, f32[32,1,4096]{2,0,1:T(8,128)}, ...) | async-done | bytes 2097168
  (549 shorter events, 214.7 us)
Async XLA Ops:
  6.5 421.4 %copy-start = (bf16[256,4096]{1,0:T(8,128)(2,1)S(1)}, bf16[256,4096]{1,0:T(8,128)(2,1)}, u32[]{:S(2)}) copy-start(bf16[256,4096]{1,0:T(8,128)(2,1)} %param.47) | copy-start | bytes 6291460
  6.5 389.8 %all-gather.14.cloned.1.call-start = ((), (), s32[]{:S(2)}) async-start(), calls=%async_computation | async-start | bytes 9437184 | tf_op jit(solution)/shard_map/all_gather | solution.py:129
  7.3 565.5 %all-gather.16.cloned.1.call-start = ((), (), s32[]{:S(2)}) async-start(), calls=%async_computation.1 | async-start | bytes 1179648 | tf_op jit(solution)/shard_map/all_gather | solution.py:22
  119.0 110.6 %copy-start.4 = (bf16[32,4096]{1,0:T(8,128)(2,1)}, bf16[32,4096]{1,0:T(8,128)(2,1)S(1)}, u32[]{:S(2)}) copy-start(bf16[32,4096]{1,0:T(8,128)(2,1)S(1)} %reshape.3902) | copy-start | bytes 786436
  234.6 86.4 %copy-start.3 = (bf16[1,32,2,64,128]{4,3,2,1,0:T(8,128)(2,1)S(1)}, bf16[1,32,2,64,128]{4,3,2,1,0:T(8,128)(2,1)}, u32[]{:S(2)}) copy-start(bf16[1,32,2,64,128]{4,3,2,1,0:T(8,128)(2,1)} %param.50) | copy-start | bytes 3145732
  242.6 35.4 %copy-start.11 = (bf16[1,32,64,2]{1,3,2,0:T(2,128)(2,1)}, bf16[1,32,64,2]{1,3,2,0:T(2,128)(2,1)S(1)}, u32[]{:S(2)}) copy-start(bf16[1,32,64,2]{1,3,2,0:T(2,128)(2,1)S(1)} %copy.1412) | copy-start | bytes 24580
  242.8 35.2 %copy-start.13 = (bf16[1,32,64,2]{1,3,2,0:T(2,128)(2,1)}, bf16[1,32,64,2]{1,3,2,0:T(2,128)(2,1)S(1)}, u32[]{:S(2)}) copy-start(bf16[1,32,64,2]{1,3,2,0:T(2,128)(2,1)S(1)} %copy.1439) | copy-start | bytes 24580
  243.6 32.9 %copy-start.15 = (bf16[1,32,64,2]{1,3,2,0:T(2,128)(2,1)}, bf16[1,32,64,2]{1,3,2,0:T(2,128)(2,1)S(1)}, u32[]{:S(2)}) copy-start(bf16[1,32,64,2]{1,3,2,0:T(2,128)(2,1)S(1)} %copy.1466) | copy-start | bytes 24580
  270.6 75.8 %copy-start.68 = (s32[32,4]{0,1:T(4,128)S(1)}, s32[32,4]{0,1:T(4,128)}, u32[]{:S(2)}) copy-start(s32[32,4]{0,1:T(4,128)} %param.51) | copy-start | bytes 1540
  307.7 20.2 %copy-start.10 = (f32[8,32,1,1,4]{4,0,1,3,2:T(8,128)S(1)}, f32[8,32,1,1,4]{4,0,1,3,2:T(8,128)}, u32[]{:S(2)}) copy-start(f32[8,32,1,1,4]{4,0,1,3,2:T(8,128)} %convolution_bitcast_fusion.10) | copy-start | bytes 12292
  307.7 39.4 %copy-start.56 = (s32[4,8,32]{2,1,0:T(8,128)S(1)}, s32[4,8,32]{2,1,0:T(8,128)}, u32[]{:S(2)}) copy-start(s32[4,8,32]{2,1,0:T(8,128)} %param.53) | copy-start | bytes 12292
  322.2 64.8 %collective-permute-start.7 = (f32[8,32,1,1,68]{4,0,1,3,2:T(8,128)}, f32[8,32,1,1,68]{4,0,1,3,2:T(8,128)}, u32[]{:S(2)}, u32[]{:S(2)}) collective-permute-start(f32[8,32,1,1,68]{4,0,1,3,2:T(8,128)} %maximum_multiply_fusion.3), channel_id=1, source_target_pairs={{0,1},{1,0},{2,3},{3,2},{4,5},{5,4},{6,7},{7,6},{8,9},{9,8},{10,11... | collective-permute-start | bytes 208904 | tf_op jit(solution)/shard_map/ppermute | solution.py:18
  325.5 63.4 %collective-permute-start.5 = (f32[8,32,1,1,68]{4,0,1,3,2:T(8,128)}, f32[8,32,1,1,68]{4,0,1,3,2:T(8,128)}, u32[]{:S(2)}, u32[]{:S(2)}) collective-permute-start(f32[8,32,1,1,68]{4,0,1,3,2:T(8,128)} %maximum_multiply_fusion.2), channel_id=1, source_target_pairs={{0,1},{1,0},{2,3},{3,2},{4,5},{5,4},{6,7},{7,6},{8,9},{9,8},{10,11... | collective-permute-start | bytes 208904 | tf_op jit(solution)/shard_map/ppermute | solution.py:18
  328.6 91.0 %collective-permute-start.3 = (f32[8,32,1,1,68]{4,0,1,3,2:T(8,128)}, f32[8,32,1,1,68]{4,0,1,3,2:T(8,128)}, u32[]{:S(2)}, u32[]{:S(2)}) collective-permute-start(f32[8,32,1,1,68]{4,0,1,3,2:T(8,128)} %maximum_multiply_fusion.1), channel_id=1, source_target_pairs={{0,1},{1,0},{2,3},{3,2},{4,5},{5,4},{6,7},{7,6},{8,9},{9,8},{10,11... | collective-permute-start | bytes 208904 | tf_op jit(solution)/shard_map/ppermute | solution.py:18
  329.5 20.5 %copy-start.17 = (bf16[1,32,64,2]{1,3,2,0:T(2,128)(2,1)}, bf16[1,32,64,2]{1,3,2,0:T(2,128)(2,1)S(1)}, u32[]{:S(2)}) copy-start(bf16[1,32,64,2]{1,3,2,0:T(2,128)(2,1)S(1)} %copy.1383) | copy-start | bytes 24580
  343.6 47.2 %collective-permute-start.1 = (f32[8,32,1,1,68]{4,0,1,3,2:T(8,128)}, f32[8,32,1,1,68]{4,0,1,3,2:T(8,128)}, u32[]{:S(2)}, u32[]{:S(2)}) collective-permute-start(f32[8,32,1,1,68]{4,0,1,3,2:T(8,128)} %maximum_multiply_fusion), channel_id=1, source_target_pairs={{0,1},{1,0},{2,3},{3,2},{4,5},{5,4},{6,7},{7,6},{8,9},{9,8},{10,11... | collective-permute-start | bytes 208904 | tf_op jit(solution)/shard_map/ppermute | solution.py:18
  362.5 16.7 %copy-start.12 = (bf16[1,32,64,2]{1,3,2,0:T(2,128)(2,1)S(1)}, bf16[1,32,64,2]{1,3,2,0:T(2,128)(2,1)}, u32[]{:S(2)}) copy-start(bf16[1,32,64,2]{1,3,2,0:T(2,128)(2,1)} %copy-done.11) | copy-start | bytes 24580
  362.5 17.4 %copy-start.14 = (bf16[1,32,64,2]{1,3,2,0:T(2,128)(2,1)S(1)}, bf16[1,32,64,2]{1,3,2,0:T(2,128)(2,1)}, u32[]{:S(2)}) copy-start(bf16[1,32,64,2]{1,3,2,0:T(2,128)(2,1)} %copy-done.13) | copy-start | bytes 24580
  362.5 18.1 %copy-start.16 = (bf16[1,32,64,2]{1,3,2,0:T(2,128)(2,1)S(1)}, bf16[1,32,64,2]{1,3,2,0:T(2,128)(2,1)}, u32[]{:S(2)}) copy-start(bf16[1,32,64,2]{1,3,2,0:T(2,128)(2,1)} %copy-done.15) | copy-start | bytes 24580
  386.4 33.4 %copy-start.20 = (pred[8,32,1,4]{3,0,1,2:T(8,128)(4,1)}, pred[8,32,1,4]{3,0,1,2:T(8,128)(4,1)S(1)}, u32[]{:S(2)}) copy-start(pred[8,32,1,4]{3,0,1,2:T(8,128)(4,1)S(1)} %compare_bitcast_fusion.2) | copy-start | bytes 3076
  410.4 15.2 %copy-start.1 = (bf16[32,4,1,128,128]{4,3,2,1,0:T(8,128)(2,1)}, bf16[32,4,1,128,128]{4,3,2,1,0:T(8,128)(2,1)S(1)}, u32[]{:S(2)}) copy-start(bf16[32,4,1,128,128]{4,3,2,1,0:T(8,128)(2,1)S(1)} %get-tuple-element.1348) | copy-start | bytes 12582916
  414.0 9.8 %copy-start.64 = (s32[32]{0:T(128)S(1)}, s32[32]{0:T(128)}, u32[]{:S(2)}) copy-start(s32[32]{0:T(128)} %param.52) | copy-start | bytes 388
  415.2 11.0 %copy-start.65 = (pred[8]{0:T(512)(128)(4,1)S(1)}, pred[8]{0:T(512)(128)(4,1)}, u32[]{:S(2)}) copy-start(pred[8]{0:T(512)(128)(4,1)} %iota_compare_fusion.2) | copy-start | bytes 28
  415.3 11.7 %copy-start.30 = (bf16[8,32,1,1,68]{4,0,1,3,2:T(8,128)(2,1)S(1)}, bf16[8,32,1,1,68]{4,0,1,3,2:T(8,128)(2,1)}, u32[]{:S(2)}) copy-start(bf16[8,32,1,1,68]{4,0,1,3,2:T(8,128)(2,1)} %copy-done.29) | copy-start | bytes 104452
  415.3 11.7 %copy-start.39 = (f32[32,128,8]{1,2,0:T(8,128)S(1)}, f32[32,128,8]{1,2,0:T(8,128)}, u32[]{:S(2)}) copy-start(f32[32,128,8]{1,2,0:T(8,128)} %fusion.43) | copy-start | bytes 393220
  415.3 5.6 collective-permute-start.6
  415.6 6.4 collective-permute-start.4
  417.6 5.5 collective-permute-start.2
  417.7 6.1 collective-permute-start
  427.9 162.4 %all-gather.18.cloned.1.call-start = ((), (), s32[]{:S(2)}) async-start(), calls=%async_computation.2 | async-start | bytes 1179648 | tf_op jit(solution)/shard_map/all_gather | solution.py:22
  441.7 161.5 %all-gather.22.cloned.1.call-start = ((), (), s32[]{:S(2)}) async-start(), calls=%async_computation.4 | async-start | bytes 1179648 | tf_op jit(solution)/shard_map/all_gather | solution.py:22
  451.2 171.3 %all-gather.20.cloned.1.call-start = ((), (), s32[]{:S(2)}) async-start(), calls=%async_computation.3 | async-start | bytes 1179648 | tf_op jit(solution)/shard_map/all_gather | solution.py:22
  458.9 112.1 %copy-start.28 = (bf16[8,32,1,1,68]{4,0,1,3,2:T(8,128)(2,1)S(1)}, bf16[8,32,1,1,68]{4,0,1,3,2:T(8,128)(2,1)}, u32[]{:S(2)}) copy-start(bf16[8,32,1,1,68]{4,0,1,3,2:T(8,128)(2,1)} %copy-done.27) | copy-start | bytes 104452
  458.9 112.1 %copy-start.38 = (f32[32,128,8]{1,2,0:T(8,128)S(1)}, f32[32,128,8]{1,2,0:T(8,128)}, u32[]{:S(2)}) copy-start(f32[32,128,8]{1,2,0:T(8,128)} %fusion.41) | copy-start | bytes 393220
  477.9 12.9 %copy-start.42 = (f32[8,8,32,1]{2,1,3,0:T(8,128)}, f32[8,8,32,1]{2,1,3,0:T(8,128)S(1)}, u32[]{:S(2)}) copy-start(f32[8,8,32,1]{2,1,3,0:T(8,128)S(1)} %all_gather.87) | copy-start | bytes 24580
  490.8 12.9 %copy-start.43 = (f32[8,8,32,1]{2,1,3,0:T(8,128)}, f32[8,8,32,1]{2,1,3,0:T(8,128)S(1)}, u32[]{:S(2)}) copy-start(f32[8,8,32,1]{2,1,3,0:T(8,128)S(1)} %all_gather.86) | copy-start | bytes 24580
  503.7 13.1 %copy-start.40 = (f32[8,8,32,1]{2,1,3,0:T(8,128)}, f32[8,8,32,1]{2,1,3,0:T(8,128)S(1)}, u32[]{:S(2)}) copy-start(f32[8,8,32,1]{2,1,3,0:T(8,128)S(1)} %all_gather.104) | copy-start | bytes 24580
  516.7 12.9 %copy-start.41 = (f32[8,8,32,1]{2,1,3,0:T(8,128)}, f32[8,8,32,1]{2,1,3,0:T(8,128)S(1)}, u32[]{:S(2)}) copy-start(f32[8,8,32,1]{2,1,3,0:T(8,128)S(1)} %all_gather.105) | copy-start | bytes 24580
  529.6 43.2 %copy-start.35 = (f32[8,8,32,1]{2,1,3,0:T(8,128)}, f32[8,8,32,1]{2,1,3,0:T(8,128)S(1)}, u32[]{:S(2)}) copy-start(f32[8,8,32,1]{2,1,3,0:T(8,128)S(1)} %all_gather.98) | copy-start | bytes 24580
  542.5 30.3 %copy-start.36 = (f32[8,8,32,1]{2,1,3,0:T(8,128)}, f32[8,8,32,1]{2,1,3,0:T(8,128)S(1)}, u32[]{:S(2)}) copy-start(f32[8,8,32,1]{2,1,3,0:T(8,128)S(1)} %all_gather.99) | copy-start | bytes 24580
  572.7 237.9 %all-reduce.9.cloned.1.call-start = ((), (), s32[]{:S(2)}) async-start(), calls=%async_computation.5 | async-start | bytes 4194304
  590.3 14.0 %copy-start.37 = (f32[8,32,1]{1,2,0:T(1,128)}, f32[8,32,1]{1,2,0:T(1,128)S(1)}, u32[]{:S(2)}) copy-start(f32[8,32,1]{1,2,0:T(1,128)S(1)} %get-tuple-element.811) | copy-start | bytes 3076
  603.1 21.0 %slice-start = ((f32[8,8,32,1]{2,1,3,0:T(8,128)}), f32[1,8,32,1]{2,1,3,0:T(8,128)S(1)}, s32[]{:S(2)}) async-start(f32[8,8,32,1]{2,1,3,0:T(8,128)} %copy-done.35), calls=%async_computation.6 | async-start | bytes 8192 | tf_op jit(solution)/shard_map/jit(dynamic_index_in_dim)/dynamic_slice | solution.py:25
  603.2 21.0 %slice-start.1 = ((f32[8,8,32,1]{2,1,3,0:T(8,128)}), f32[1,8,32,1]{2,1,3,0:T(8,128)S(1)}, s32[]{:S(2)}) async-start(f32[8,8,32,1]{2,1,3,0:T(8,128)} %copy-done.36), calls=%async_computation.7 | async-start | bytes 8192 | tf_op jit(solution)/shard_map/jit(dynamic_index_in_dim)/dynamic_slice | solution.py:25
  620.7 30.2 %copy-start.2 = (bf16[128,4096]{1,0:T(8,128)(2,1)S(1)}, bf16[128,4096]{1,0:T(8,128)(2,1)}, u32[]{:S(2)}) copy-start(bf16[128,4096]{1,0:T(8,128)(2,1)} %param.44) | copy-start | bytes 3145732
  624.2 29.0 %copy-start.69 = (f32[32]{0:T(128)S(1)}, f32[32]{0:T(128)}, u32[]{:S(2)}) copy-start(f32[32]{0:T(128)} %fusion.263) | copy-start | bytes 388
  655.4 155.2 %copy-start.6 = (bf16[4,1,1,4096]{3,0,2,1:T(4,128)(2,1)S(1)}, bf16[4,1,1,4096]{3,0,2,1:T(4,128)(2,1)}, u32[]{:S(2)}) copy-start(bf16[4,1,1,4096]{3,0,2,1:T(4,128)(2,1)} %param.40) | copy-start | bytes 98308
  655.4 155.2 %copy-start.57 = (f32[4096]{0:T(1024)S(1)}, f32[4096]{0:T(1024)}, u32[]{:S(2)}) copy-start(f32[4096]{0:T(1024)} %param.48) | copy-start | bytes 49156
  (39 other events, 169.1 us)
Sparse Core Ops, SparseCore 0:
  9.2 54.3 all-gather.13
  428.0 22.2 all-gather.15
  452.1 26.7 all-gather.17
  480.7 26.8 all-gather.21
  572.8 22.2 all-gather.19
  658.6 151.9 all-reduce.8
where the time goes:
time: 834 us; the launch traced here: 820 us
  blocking collectives  351 us (42%)
  waiting for transfers between devices  155 us (19%)
  local copies, waits for them, and re-layouts  150 us (18%)
  other arithmetic  73.5 us (9%)
  matrix products  59.8 us (7%)
  between operations  20.3 us (2%)
  starting transfers between devices  9 us (1%)
    all_gather x4, blocking collectives, on_device(): gathered_rows = lax.all_gather(normed, 'tensor', axis=1, tiled=True)  196 us
    unnamed x7, waiting for transfers between devices  152 us
    all_gather x8, blocking collectives, joined_2(): gathered = jax.tree.map(lambda a: lax.all_gather(a, axis), part)  103 us
    all_gather x4, blocking collectives, on_device(): queries_all = lax.all_gather(queries, 'batch', axis=0, tiled=True)  51.7 us
    dynamic_slice x98, local copies, waits for them, and re-layouts, take(): lax.dynamic_index_in_dim(a, source, 0, False)  44.8 us
    add x28, other arithmetic, combine(): mixture_one * factor_one[..., None] + mixture_two * factor_two[..., None]  29.2 us
    unnamed x160, local copies, waits for them, and re-layouts  21.6 us
  transfers between devices with their start and end apart: 14, of which 4 were waited for; matrix products, arithmetic and copies ran while one was open for 29% of the time, Pallas kernels for 0%

commit v1 on v0

v1 whole, which is shorter than its diff:
```python
import math

import jax
import jax.numpy as jnp
from jax import lax
from jax.sharding import PartitionSpec as P

HDIM = 256
ROT = 64
BEAMS = 8

NEG_FILL = -1e30


def partner(value, axis, bit):
    return lax.ppermute(value, axis, [(i, i ^ 1 << bit) for i in range(lax.axis_size(axis))])


def normalize(row_block, norm_gain, norm_bias):
    widened = row_block.astype(jnp.float32)
    center = jnp.mean(widened, axis=-1, keepdims=True)
    shifted = widened - center
    variance = jnp.mean(shifted * shifted, axis=-1, keepdims=True)
    return shifted * lax.rsqrt(variance + 1e-05) * norm_gain + norm_bias


def rotate_local(vectors, position, first_column):
    half_count = vectors.shape[-1] // 2
    doubled = (first_column + 2 * jnp.arange(half_count)) % HDIM
    exponent = doubled.astype(jnp.float32) / ROT
    frequency = jnp.where(doubled < ROT, jnp.exp(-exponent * math.log(10000.0)), 0.0)
    angles = position[..., None] * frequency
    cosine = jnp.cos(angles)
    sine_part = jnp.sin(angles)
    halves = vectors.reshape(vectors.shape[:-1] + (half_count, 2))
    even_part = halves[..., 0]
    odd_part = halves[..., 1]
    turned = jnp.stack(
        [even_part * cosine - odd_part * sine_part, odd_part * cosine + even_part * sine_part],
        axis=-1,
    )
    return turned.reshape(vectors.shape)


def on_device(
    inputs,
    norm_gain,
    norm_bias,
    qkv_weight,
    out_weight,
    in_weight,
    in_bias,
    down_weight,
    down_bias,
    page_pool,
    old_cache,
    page_table,
    prompt_length,
    parents,
):
    batch_index = lax.axis_index("batch")
    tensor_index = lax.axis_index("tensor")
    groups = lax.axis_size("batch")
    steps = inputs.shape[0]
    model_width = inputs.shape[3]
    columns = qkv_weight.shape[2]
    requests = page_table.shape[0]
    history = old_cache.shape[3]
    page_count = page_table.shape[1]
    page_size = page_pool.shape[2]
    pool_dev = page_pool.shape[0]
    prompt_span = page_count * page_size
    local_reqs = requests // groups
    scale_factor = HDIM ** (-0.5)
    first_column = tensor_index * columns

    normed = normalize(inputs[:, 0], norm_gain, norm_bias).astype(jnp.bfloat16)
    rows = lax.all_gather(normed, "tensor", axis=1, tiled=True)
    flat = rows.reshape(steps * requests, model_width)
    qkv_flat = qkv_weight.reshape(model_width, 3 * columns)
    projected = jnp.dot(flat, qkv_flat, preferred_element_type=jnp.float32).reshape(
        steps, requests, 3 * columns
    )
    ffn = jnp.dot(flat, in_weight, preferred_element_type=jnp.float32).reshape(
        steps, requests, -1
    )
    hidden = jax.nn.gelu(ffn + in_bias, approximate=True).astype(jnp.bfloat16)

    position = (
        prompt_length[None, :] + history + jnp.arange(steps, dtype=jnp.int32)[:, None]
    ).astype(jnp.float32)
    queries = rotate_local(projected[..., :columns], position, first_column).astype(jnp.bfloat16)
    fresh_keys = rotate_local(
        projected[..., columns : 2 * columns], position, first_column
    ).astype(jnp.bfloat16)
    fresh_values = projected[..., 2 * columns :].astype(jnp.bfloat16)

    query_all = lax.all_gather(queries[:, None], "batch", axis=1, tiled=True)

    beam_ids = jnp.broadcast_to(jnp.arange(BEAMS, dtype=jnp.int32)[:, None], (BEAMS, requests))
    new_ok_steps = []
    old_ok_steps = []
    for step_index in range(steps):
        lineage = beam_ids
        per_t = [None] * steps
        for back_step in range(step_index, -1, -1):
            per_t[back_step] = lineage == batch_index
            lineage = jnp.take_along_axis(parents[back_step], lineage, axis=0)
        for t in range(step_index + 1, steps):
            per_t[t] = jnp.zeros((BEAMS, requests), bool)
        new_ok_steps.append(jnp.stack(per_t, axis=-1))
        old_ok_steps.append(lineage == batch_index)
    new_ok = jnp.stack(new_ok_steps, axis=0)
    old_ok = jnp.stack(old_ok_steps, axis=0)

    old_keys = old_cache[0, :, 0]
    old_values = old_cache[0, :, 1]
    old_scores = jnp.einsum(
        "sbrc,rhc->sbrh", query_all, old_keys, preferred_element_type=jnp.float32
    )
    new_scores = jnp.einsum(
        "sbrc,trc->sbrt", query_all, fresh_keys, preferred_element_type=jnp.float32
    )

    query_local = lax.dynamic_index_in_dim(
        query_all.reshape(steps, BEAMS, local_reqs, groups, columns), batch_index, 3, False
    )
    table_local = lax.dynamic_index_in_dim(
        page_table.reshape(local_reqs, groups, page_count), batch_index, 1, False
    ) - batch_index * pool_dev
    table_local = jnp.clip(table_local, 0, pool_dev - 1)
    length_local = lax.dynamic_index_in_dim(
        prompt_length.reshape(local_reqs, groups), batch_index, 1, False
    )
    pages = page_pool[table_local]
    prompt_keys = pages[:, :, 0].reshape(local_reqs, prompt_span, columns)
    prompt_values = pages[:, :, 1].reshape(local_reqs, prompt_span, columns)
    prompt_scores = jnp.einsum(
        "sbrc,rtc->sbrt", query_local, prompt_keys, preferred_element_type=jnp.float32
    )

    other = partner((old_scores, new_scores, prompt_scores), "tensor", 0)
    old_scores = (old_scores + other[0]) * scale_factor
    new_scores = (new_scores + other[1]) * scale_factor
    prompt_scores = (prompt_scores + other[2]) * scale_factor

    old_mask = old_ok[..., None]
    old_masked = jnp.where(old_mask, old_scores, NEG_FILL)
    new_masked = jnp.where(new_ok, new_scores, NEG_FILL)
    chain_peak = jnp.maximum(jnp.max(old_masked, axis=-1), jnp.max(new_masked, axis=-1))
    old_w = jnp.where(old_mask, jnp.exp(old_masked - chain_peak[..., None]), 0.0)
    new_w = jnp.where(new_ok, jnp.exp(new_masked - chain_peak[..., None]), 0.0)
    chain_total = jnp.sum(old_w, axis=-1) + jnp.sum(new_w, axis=-1)
    chain_mix = jnp.einsum(
        "sbrh,rhc->sbrc", old_w.astype(jnp.bfloat16), old_values, preferred_element_type=jnp.float32
    ) + jnp.einsum(
        "sbrt,trc->sbrc",
        new_w.astype(jnp.bfloat16),
        fresh_values,
        preferred_element_type=jnp.float32,
    )

    prompt_mask = (jnp.arange(prompt_span)[None, :] < length_local[:, None])[None, None]
    prompt_masked = jnp.where(prompt_mask, prompt_scores, NEG_FILL)
    prompt_peak = jnp.max(prompt_masked, axis=-1)
    prompt_w = jnp.where(prompt_mask, jnp.exp(prompt_masked - prompt_peak[..., None]), 0.0)
    prompt_total = jnp.sum(prompt_w, axis=-1)
    prompt_mix = jnp.einsum(
        "sbrt,rtc->sbrc",
        prompt_w.astype(jnp.bfloat16),
        prompt_values,
        preferred_element_type=jnp.float32,
    )

    slot_hit = (jnp.arange(groups) == batch_index)[None, None, None, :]
    def spread(values, fill):
        placed = jnp.where(slot_hit, values[..., None], fill)
        return placed.reshape(values.shape[:2] + (requests,))

    def spread_mix(values):
        placed = jnp.where(slot_hit[..., None], values[:, :, :, None, :], 0.0)
        return placed.reshape(values.shape[:2] + (requests, columns))

    p_peak = spread(prompt_peak, NEG_FILL)
    p_total = spread(prompt_total, 0.0)
    p_mix = spread_mix(prompt_mix)
    peak = jnp.maximum(chain_peak, p_peak)
    f_chain = jnp.exp(chain_peak - peak)
    f_prompt = jnp.exp(p_peak - peak)
    total = chain_total * f_chain + p_total * f_prompt
    mix = chain_mix * f_chain[..., None] + p_mix * f_prompt[..., None]

    packed = jnp.concatenate([mix, peak[..., None], total[..., None]], axis=-1)
    received = lax.all_to_all(packed, "batch", 1, 1, tiled=True)
    r_mix = received[..., :columns]
    r_peak = received[..., columns]
    r_total = received[..., columns + 1]
    g_peak = jnp.max(r_peak, axis=1, keepdims=True)
    factor = jnp.exp(r_peak - g_peak)
    all_total = jnp.sum(r_total * factor, axis=1)
    all_mix = jnp.sum(r_mix * factor[..., None], axis=1)
    attention = (all_mix / all_total[..., None]).astype(jnp.bfloat16)

    update = jnp.einsum(
        "src,cd->rsd", attention, out_weight, preferred_element_type=jnp.float32
    ) + jnp.einsum("srf,fd->rsd", hidden, down_weight, preferred_element_type=jnp.float32)
    summed = lax.psum_scatter(update, "tensor", scatter_dimension=0, tiled=True)
    result = inputs[:, 0].astype(jnp.float32) + jnp.transpose(summed, (1, 0, 2)) + down_bias
    return result[:, None]


def solution(mesh):
    in_specs = (
        P(None, "batch", "tensor", None),
        P(),
        P(),
        P(None, None, "tensor"),
        P("tensor", None),
        P(None, "tensor"),
        P("tensor"),
        P("tensor", None),
        P(),
        P("batch", None, None, "tensor"),
        P("batch", None, None, None, "tensor"),
        P(),
        P(),
        P(),
    )
    out_specs = P(None, "batch", "tensor", None)
    return jax.shard_map(
        on_device, mesh=mesh, in_specs=in_specs, out_specs=out_specs, check_vma=False
    )
```

time: 834 us -> 360 us (0.43); the launches traced: 820 us -> 359 us
  blocking collectives: 351 us -> 31.7 us
  local copies, waits for them, and re-layouts: 150 us -> 52.6 us
  waiting for transfers between devices: 155 us -> 222 us
  other arithmetic: 73.5 us -> 17 us
  matrix products: 59.8 us -> 18.8 us
    all_gather x16 -> x1, blocking collectives: 351 us -> 12.8 us  [on_device(): query_all = lax.all_gather(queries[:, None], 'batch', axis=1, tiled=True)]
    all_gather x5 -> x1, waiting for transfers between devices: 0.06 us -> 53.7 us  [on_device(): rows = lax.all_gather(normed, 'tensor', axis=1, tiled=True)]
    dynamic_slice x98 -> x3, local copies, waits for them, and re-layouts: 44.8 us -> 0.34 us  [the longest x1 0.19 us: on_device(): lax.dynamic_index_in_dim(prompt_length.reshape(local_reqs, groups), batch...]
    dot_general x36 -> x7, matrix products: 59.8 us -> 16.2 us  [the longest x1 4.97 us: on_device(): jnp.einsum('srf,fd->rsd', hidden, down_weight, preferred_element_type=jnp...]
    add x57 -> x3, other arithmetic: 30.3 us -> 2.15 us  [the longest x1 1.51 us: on_device(): inputs[:, 0].astype(jnp.float32) + jnp.transpose(summed, (1, 0, 2))]
    all_to_all x0 -> x1, blocking collectives: none -> 18.9 us  [on_device(): received = lax.all_to_all(packed, 'batch', 1, 1, tiled=True)]
    ppermute x8 -> x3, waiting for transfers between devices: 2.92 us -> 18.2 us  [partner(): lax.ppermute(value, axis, [(i, i ^ 1 << bit) for i in range(lax.axis_size...]
    unnamed x160 -> x42, local copies, waits for them, and re-layouts: 21.6 us -> 10.5 us
  transfers between devices with their start and end apart: 14 -> 5, of which waited for: 4 -> 5; matrix products, arithmetic and copies ran while one was open for 29% -> 8% of each run, Pallas kernels for 0% -> 0%
where the time goes in v1:
time: 360 us; the launch traced here: 359 us
  waiting for transfers between devices  222 us (62%)
  local copies, waits for them, and re-layouts  52.6 us (15%)
  blocking collectives  31.7 us (9%)
  matrix products  18.8 us (5%)
  other arithmetic  17 us (5%)
  between operations  13.9 us (4%)
    unnamed x3, waiting for transfers between devices  150 us
    all_gather x1, waiting for transfers between devices, on_device(): rows = lax.all_gather(normed, 'tensor', axis=1, tiled=True)  53.7 us
    all_to_all x1, blocking collectives, on_device(): received = lax.all_to_all(packed, 'batch', 1, 1, tiled=True)  18.9 us
    ppermute x3, waiting for transfers between devices, partner(): lax.ppermute(value, axis, [(i, i ^ 1 << bit) for i in range(lax.axis_size...  18.2 us
    gather x27, local copies, waits for them, and re-layouts, on_device(): lineage = jnp.take_along_axis(parents[back_step], lineage, axis=0)  15.6 us
    all_gather x1, blocking collectives, on_device(): query_all = lax.all_gather(queries[:, None], 'batch', axis=1, tiled=True)  12.8 us
    unnamed x42, local copies, waits for them, and re-layouts  10.5 us
  transfers between devices with their start and end apart: 5, of which 5 were waited for; matrix products, arithmetic and copies ran while one was open for 8% of the time, Pallas kernels for 0%

profile of v1, /device:TPU:2, one launch (start us, length us, event | category | flops | bytes accessed | tf_op | source)
XLA Modules:
  0.0 358.6 jit_solution(18365220035608578066)
XLA Ops:
  6.5 1.1 convert_reduce_fusion
  8.6 1.5 fusion.85
  11.0 1.4 gather_fusion.7
  12.6 1.4 gather_fusion.4
  14.0 1.4 gather_fusion.8
  15.7 1.4 gather_fusion.2
  17.1 1.4 gather_fusion.9
  18.7 1.4 gather_fusion.1
  20.1 1.4 gather_fusion.10
  21.9 1.4 gather_fusion.5
  23.5 1.4 gather_fusion.6
  25.2 1.4 gather_fusion.3
  27.2 4.7 %copy.447 = bf16[4096,3,128]{0,2,1:T(8,128)(2,1)} copy(bf16[4096,3,128]{2,0,1:T(8,128)(2,1)} %param.19) | data formatting | bytes 6291456 | tf_op args[3]
  32.9 2.0 gather_fusion
  35.0 1.1 fusion.126
  36.0 53.7 %all-gather.2.cloned.1.call-done = bf16[4,32,4096]{2,0,1:T(4,128)(2,1)} async-done(((bf16[4,1,4096]{2,0,1:T(4,128)(2,1)}), bf16[4,32,4096]{2,0,1:T(4,128)(2,1)}) %all-gather.2.cloned.1.call-update) | async-done | bytes 1048592 | tf_op jit(solution)/shard_map/all_gather | solution.py:78
  89.7 3.4 fusion.13
  95.4 12.8 %all_gather.7 = bf16[4,8,32,128]{3,2,0,1:T(8,128)(2,1)S(1)} all-gather(bf16[4,1,32,128]{3,2,0,1:T(8,128)(2,1)S(1)} %copy.454), channel_id=1, replica_groups=mesh['batch'=8,'tensor'=32] {'batch'}, dimensions={1}, use_global_device_ids=true | all-gather | bytes 294912 | tf_op jit(solution)/shard_map/all_gather | solution.py:98
  108.5 1.3 convolution_bitcast_fusion.4
  110.3 1.4 convolution_bitcast_fusion.2
  111.8 1.5 collective-permute-start
  113.4 1.3 convolution_bitcast_fusion.3
  115.5 3.4 collective-permute-done.1
  119.9 10.2 %collective-permute-done = f32[4,8,32,64]{3,1,0,2:T(8,128)S(1)} collective-permute-done((f32[4,8,32,64]{3,1,0,2:T(8,128)S(1)}, f32[4,8,32,64]{3,1,0,2:T(8,128)S(1)}, u32[]{:S(2)}, u32[]{:S(2)}) %collective-permute-start) | collective-permute-done | bytes 262176 | tf_op jit(solution)/shard_map/ppermute | solution.py:16
  130.6 4.6 %collective-permute-done.2 = f32[4,8,4,512]{3,1,0,2:T(8,128)S(1)} collective-permute-done((f32[4,8,4,512]{3,1,0,2:T(8,128)S(1)}, f32[4,8,4,512]{3,1,0,2:T(8,128)S(1)}, u32[]{:S(2)}, u32[]{:S(2)}) %collective-permute-start.2) | collective-permute-done | bytes 262176 | tf_op jit(solution)/shard_map/ppermute | solution.py:16
  138.2 1.3 fusion.31
  139.5 1.6 fusion.21
  141.7 1.5 copy.478
  144.0 1.4 copy.479
  145.4 1.4 broadcast_in_dim.189
  146.8 1.5 broadcast_in_dim.190
  148.3 1.4 broadcast_in_dim.178
  149.8 1.5 broadcast_in_dim.187
  151.3 1.4 bitcast_maximum_fusion
  152.7 2.0 copy.481
  154.7 2.0 copy.482
  156.6 1.3 convolution_bitcast_fusion.5
  158.0 1.1 fusion.18
  159.1 1.7 convolution_bitcast_fusion.1
  162.6 18.9 %all_to_all.5 = f32[4,8,32,130]{3,0,2,1:T(4,128)S(1)} all-to-all(f32[4,8,32,130]{3,0,2,1:T(4,128)S(1)} %copy.483), channel_id=1, replica_groups=mesh['batch'=8,'tensor'=32] {'batch'}, dimensions={1} | all-to-all | bytes 1064960 | tf_op jit(solution)/shard_map/all_to_all | solution.py:194
  181.5 1.4 fusion.125
  182.9 1.3 copy.516
  184.2 1.3 copy.517
  186.4 3.0 fusion.10
  189.4 5.0 %fusion = f32[32,4,4096]{2,0,1:T(8,128)} fusion(f32[4,32,4096]{2,1,0:T(8,128)} %fusion.10, bf16[256,4096]{1,0:T(8,128)(2,1)S(1)} %copy-done, bf16[4096,256]{1,0:T(8,128)(2,1)} %param.21, bf16[4,32,4096]{2,0,1:T(4,128)(2,1)S(1)} %copy-done.1, f32[256]{0:T(256)S(1)} %copy-done.13), kind=kOutput, calls=%fused_computation.12 | convolution fusion | flops 537722880 | bytes 9438208 | tf_op jit(solution)/shard_map/srf,fd->rsd/dot_general | solution.py:206
  194.4 4.3 %copy.491 = f32[32,4,4096]{2,1,0:T(4,128)} copy(f32[32,4,4096]{2,0,1:T(8,128)} %fusion) | data formatting | bytes 4194304 | tf_op jit(solution)/shard_map/add | solution.py:204
  199.9 149.7 %all-reduce.3.cloned.1.call-done = f32[32,4,4096]{2,1,0:T(4,128)} async-done(((f32[32,4,4096]{2,1,0:T(4,128)}), f32[32,4,4096]{2,1,0:T(4,128)}) %all-reduce.3.cloned.1.call-update) | async-done | bytes 2097168
  349.6 1.5 fusion.86
  (131 shorter events, 19.1 us)
Async XLA Ops:
  6.5 182.9 %copy-start = (bf16[256,4096]{1,0:T(8,128)(2,1)S(1)}, bf16[256,4096]{1,0:T(8,128)(2,1)}, u32[]{:S(2)}) copy-start(bf16[256,4096]{1,0:T(8,128)(2,1)} %param.23) | copy-start | bytes 6291460
  6.5 83.1 %all-gather.2.cloned.1.call-start = ((), (), s32[]{:S(2)}) async-start(), calls=%async_computation.1 | async-start | bytes 1081344 | tf_op jit(solution)/shard_map/all_gather | solution.py:78
  10.1 339.5 %all-reduce.3.cloned.1.call-start = ((), (), s32[]{:S(2)}) async-start(), calls=%async_computation.2 | async-start | bytes 4194304
  27.2 4.9 %copy-start.12 = (s32[32,4]{0,1:T(4,128)S(1)}, s32[32,4]{0,1:T(4,128)}, u32[]{:S(2)}) copy-start(s32[32,4]{0,1:T(4,128)} %param.27) | copy-start | bytes 1540
  27.2 5.2 %copy-start.14 = (s32[32]{0:T(128)S(1)}, s32[32]{0:T(128)}, u32[]{:S(2)}) copy-start(s32[32]{0:T(128)} %param.28) | copy-start | bytes 388
  32.1 98.1 %copy-start.8 = (pred[4,8,32]{1,0,2:T(4,128)(4,1)}, pred[4,8,32]{1,0,2:T(4,128)(4,1)S(1)}, u32[]{:S(2)}) copy-start(pred[4,8,32]{1,0,2:T(4,128)(4,1)S(1)} %copy.446) | copy-start | bytes 3076
  109.7 9.2 %collective-permute-start.1 = (f32[4,8,32,4]{1,3,0,2:T(4,128)S(1)}, f32[4,8,32,4]{1,3,0,2:T(4,128)S(1)}, u32[]{:S(2)}, u32[]{:S(2)}) collective-permute-start(f32[4,8,32,4]{1,3,0,2:T(4,128)S(1)} %convolution_bitcast_fusion.4), channel_id=1, source_target_pairs={{0,1},{1,0},{2,3},{3,2},{4,5},{5,4},{6,7},{7,6},{8,9},{9,8},{10,11... | collective-permute-start | bytes 49160 | tf_op jit(solution)/shard_map/ppermute | solution.py:16
  111.8 18.4 %collective-permute-start = (f32[4,8,32,64]{3,1,0,2:T(8,128)S(1)}, f32[4,8,32,64]{3,1,0,2:T(8,128)S(1)}, u32[]{:S(2)}, u32[]{:S(2)}) collective-permute-start(f32[4,8,32,64]{3,1,0,2:T(8,128)S(1)} %convolution_bitcast_fusion.2), channel_id=1, source_target_pairs={{0,1},{1,0},{2,3},{3,2},{4,5},{5,4},{6,7},{7,6},{8,9},{9,8},{10,11... | collective-permute-start | bytes 786440 | tf_op jit(solution)/shard_map/ppermute | solution.py:16
  114.7 20.5 %collective-permute-start.2 = (f32[4,8,4,512]{3,1,0,2:T(8,128)S(1)}, f32[4,8,4,512]{3,1,0,2:T(8,128)S(1)}, u32[]{:S(2)}, u32[]{:S(2)}) collective-permute-start(f32[4,8,4,512]{3,1,0,2:T(8,128)S(1)} %convolution_bitcast_fusion.3), channel_id=1, source_target_pairs={{0,1},{1,0},{2,3},{3,2},{4,5},{5,4},{6,7},{7,6},{8,9},{9,8},{10,11... | collective-permute-start | bytes 786440 | tf_op jit(solution)/shard_map/ppermute | solution.py:16
  118.9 0.7 copy-start.5
  130.2 5.0 %copy-start.4 = (f32[4,8,32,64]{3,1,0,2:T(8,128)}, f32[4,8,32,64]{3,1,0,2:T(8,128)S(1)}, u32[]{:S(2)}) copy-start(f32[4,8,32,64]{3,1,0,2:T(8,128)S(1)} %collective-permute-done) | copy-start | bytes 786436
  159.0 1.8 copy-start.6
  159.0 1.8 copy-start.9
  159.1 1.8 copy-start.10
  160.8 1.0 copy-start.2
  160.8 1.2 copy-start.3
  185.6 3.8 %copy-start.13 = (f32[256]{0:T(256)S(1)}, f32[256]{0:T(256)}, u32[]{:S(2)}) copy-start(f32[256]{0:T(256)} %param.22) | copy-start | bytes 3076
  186.2 3.2 copy-start.1
  198.7 0.7 copy-start.15
  198.7 150.9 %copy-start.7 = (bf16[4,1,1,4096]{3,0,2,1:T(4,128)(2,1)S(1)}, bf16[4,1,1,4096]{3,0,2,1:T(4,128)(2,1)}, u32[]{:S(2)}) copy-start(bf16[4,1,1,4096]{3,0,2,1:T(4,128)(2,1)} %param.16) | copy-start | bytes 98308
  198.7 150.9 %copy-start.11 = (f32[4096]{0:T(1024)S(1)}, f32[4096]{0:T(1024)}, u32[]{:S(2)}) copy-start(f32[4096]{0:T(1024)} %param.24) | copy-start | bytes 49156
Sparse Core Ops, SparseCore 0:
  10.2 79.4 all-gather.1
  198.8 150.7 all-reduce.2

commit v2 on v1

--- a/solution.py
+++ b/solution.py
@@ -10,10 +10,47 @@
 BEAMS = 8
 
 NEG_FILL = -1e30
+SCATTER_ORDER = (0, 3, 1, 4, 2)
+GATHER_ORDER = (2, 4, 1, 3, 0)
 
 
 def partner(value, axis, bit):
     return lax.ppermute(value, axis, [(i, i ^ 1 << bit) for i in range(lax.axis_size(axis))])
+
+
+def tree_reduce_scatter(x, axis, order):
+    n = x.shape[0]
+    nbits = n.bit_length() - 1
+    me = lax.axis_index(axis)
+    x = x.reshape((2,) * nbits + x.shape[1:])
+    remaining = list(range(nbits - 1, -1, -1))
+    for k in order:
+        a = remaining.index(k)
+        bit = (me >> k) & 1
+        keep = lax.dynamic_index_in_dim(x, bit, a, keepdims=False)
+        send = lax.dynamic_index_in_dim(x, 1 - bit, a, keepdims=False)
+        x = keep + partner(send, axis, k)
+        remaining.pop(a)
+    return x
+
+
+def tree_all_gather(x, axis, order, out_axis):
+    n = lax.axis_size(axis)
+    nbits = n.bit_length() - 1
+    me = lax.axis_index(axis)
+    have = []
+    for k in order:
+        bit = (me >> k) & 1
+        got = partner(x, axis, k)
+        low = jnp.where(bit == 0, x, got)
+        high = jnp.where(bit == 0, got, x)
+        x = jnp.stack([low, high], axis=0)
+        have.insert(0, k)
+    rest = list(range(nbits, x.ndim))
+    lead = [have.index(b) for b in range(nbits - 1, -1, -1)]
+    perm = rest[:out_axis] + lead + rest[out_axis:]
+    x = jnp.transpose(x, perm)
+    return x.reshape(x.shape[:out_axis] + (n,) + x.shape[out_axis + nbits :])
 
 
 def normalize(row_block, norm_gain, norm_bias):
@@ -75,7 +112,7 @@
     first_column = tensor_index * columns
 
     normed = normalize(inputs[:, 0], norm_gain, norm_bias).astype(jnp.bfloat16)
-    rows = lax.all_gather(normed, "tensor", axis=1, tiled=True)
+    rows = tree_all_gather(normed[:, 0], "tensor", GATHER_ORDER, 1)
     flat = rows.reshape(steps * requests, model_width)
     qkv_flat = qkv_weight.reshape(model_width, 3 * columns)
     projected = jnp.dot(flat, qkv_flat, preferred_element_type=jnp.float32).reshape(
@@ -105,7 +142,8 @@
         per_t = [None] * steps
         for back_step in range(step_index, -1, -1):
             per_t[back_step] = lineage == batch_index
-            lineage = jnp.take_along_axis(parents[back_step], lineage, axis=0)
+            pick = lineage[:, None, :] == jnp.arange(BEAMS, dtype=jnp.int32)[None, :, None]
+            lineage = jnp.sum(jnp.where(pick, parents[back_step][None], 0), axis=1)
         for t in range(step_index + 1, steps):
             per_t[t] = jnp.zeros((BEAMS, requests), bool)
         new_ok_steps.append(jnp.stack(per_t, axis=-1))
@@ -204,8 +242,8 @@
     update = jnp.einsum(
         "src,cd->rsd", attention, out_weight, preferred_element_type=jnp.float32
     ) + jnp.einsum("srf,fd->rsd", hidden, down_weight, preferred_element_type=jnp.float32)
-    summed = lax.psum_scatter(update, "tensor", scatter_dimension=0, tiled=True)
-    result = inputs[:, 0].astype(jnp.float32) + jnp.transpose(summed, (1, 0, 2)) + down_bias
+    summed = tree_reduce_scatter(update, "tensor", SCATTER_ORDER)
+    result = inputs[:, 0].astype(jnp.float32) + summed[:, None] + down_bias
     return result[:, None]
 
 

time: 360 us -> 256 us (0.71)
  waiting for transfers between devices: 222 us -> 95.5 us
  starting transfers between devices: 3.01 us -> 37.8 us
  blocking collectives: 31.7 us -> 13.3 us
  other arithmetic: 17 us -> 30.4 us
  between operations: 13.9 us -> 0.58 us
  local copies, waits for them, and re-layouts: 52.6 us -> 58.2 us
    unnamed x3 -> x0, waiting for transfers between devices: 150 us -> none
    ppermute x3 -> x13, waiting for transfers between devices: 18.2 us -> 80.9 us  [partner(): lax.ppermute(value, axis, [(i, i ^ 1 << bit) for i in range(lax.axis_size...]
    all_gather x1 -> x0, waiting for transfers between devices: 53.7 us -> none  [on_device(): rows = lax.all_gather(normed, 'tensor', axis=1, tiled=True)]
    ppermute x3 -> x13, starting transfers between devices: 2.97 us -> 32.9 us  [partner(): lax.ppermute(value, axis, [(i, i ^ 1 << bit) for i in range(lax.axis_size...]
    all_to_all x1 -> x0, blocking collectives: 18.9 us -> none  [on_device(): received = lax.all_to_all(packed, 'batch', 1, 1, tiled=True)]
    gather x27 -> x0, local copies, waits for them, and re-layouts: 15.6 us -> none  [on_device(): lineage = jnp.take_along_axis(parents[back_step], lineage, axis=0)]
    all_to_all x0 -> x1, waiting for transfers between devices: none -> 14.6 us  [on_device(): received = lax.all_to_all(packed, 'batch', 1, 1, tiled=True)]
    dynamic_slice x0 -> x2, local copies, waits for them, and re-layouts: none -> 6.12 us  [the longest x1 4.42 us: tree_reduce_scatter(): keep = lax.dynamic_index_in_dim(x, bit, a, keepdims=False)]
  transfers between devices with their start and end apart: 5 -> 14, of which waited for: 5 -> 13; matrix products, arithmetic and copies ran while one was open for 8% -> 6% of each run, Pallas kernels for 0% -> 0%
where the time goes in v2:
time: 256 us; the launch traced here: 253 us
  waiting for transfers between devices  95.5 us (37%)
  local copies, waits for them, and re-layouts  58.2 us (23%)
  starting transfers between devices  37.8 us (15%)
  other arithmetic  30.4 us (12%)
  matrix products  17.5 us (7%)
  blocking collectives  13.3 us (5%)
    ppermute x13, waiting for transfers between devices, partner(): lax.ppermute(value, axis, [(i, i ^ 1 << bit) for i in range(lax.axis_size...  80.9 us
    ppermute x13, starting transfers between devices, partner(): lax.ppermute(value, axis, [(i, i ^ 1 << bit) for i in range(lax.axis_size...  32.9 us
    unnamed x59, local copies, waits for them, and re-layouts  15.6 us
    all_to_all x1, waiting for transfers between devices, on_device(): received = lax.all_to_all(packed, 'batch', 1, 1, tiled=True)  14.6 us
    all_gather x1, blocking collectives, on_device(): query_all = lax.all_gather(queries[:, None], 'batch', axis=1, tiled=True)  13.3 us
    broadcast_in_dim x6, local copies, waits for them, and re-layouts, spread(): placed = jnp.where(slot_hit, values[..., None], fill)  6.59 us
  transfers between devices with their start and end apart: 14, of which 13 were waited for; matrix products, arithmetic and copies ran while one was open for 6% of the time, Pallas kernels for 0%

profile of v2, /device:TPU:2, one launch (start us, length us, event | category | flops | bytes accessed | tf_op | source)
XLA Modules:
  0.0 253.2 jit_solution(8533672520904345463)
XLA Ops:
  2.9 7.3 %collective-permute-start = (bf16[4,4096]{1,0:T(4,128)(2,1)S(1)}, bf16[4,4096]{1,0:T(4,128)(2,1)S(1)}, u32[]{:S(2)}, u32[]{:S(2)}) collective-permute-start(bf16[4,4096]{1,0:T(4,128)(2,1)S(1)} %fusion.65), channel_id=1, source_target_pairs={{0,4},{1,5},{2,6},{3,7},{4,0},{5,1},{6,2},{7,3},{8,12},{9,13},{10,... | collective-permute-start | bytes 98312 | tf_op jit(solution)/shard_map/ppermute | solution.py:18
  13.4 3.3 %collective-permute-start.1 = (bf16[2,4,4096]{2,1,0:T(4,128)(2,1)S(1)}, bf16[2,4,4096]{2,1,0:T(4,128)(2,1)S(1)}, u32[]{:S(2)}, u32[]{:S(2)}) collective-permute-start(bf16[2,4,4096]{2,1,0:T(4,128)(2,1)S(1)} %pad_maximum_fusion.4), channel_id=1, source_target_pairs={{0,16},{1,17},{2,18},{3,19},{4,20},{5,21},{6,22},{7,23},{8,24},{9,... | collective-permute-start | bytes 196616 | tf_op jit(solution)/shard_map/ppermute | solution.py:18
  17.4 1.8 collective-permute-done.1
  19.4 1.9 collective-permute-start.2
  21.3 5.7 %collective-permute-done.2 = bf16[2,2,4,4096]{3,2,1,0:T(4,128)(2,1)S(1)} collective-permute-done((bf16[2,2,4,4096]{3,2,1,0:T(4,128)(2,1)S(1)}, bf16[2,2,4,4096]{3,2,1,0:T(4,128)(2,1)S(1)}, u32[]{:S(2)}, u32[]{:S(2)}) %collective-permute-start.2) | collective-permute-done | bytes 131104 | tf_op jit(solution)/shard_map/ppermute | solution.py:18
  27.4 1.7 collective-permute-start.3
  29.6 4.2 %collective-permute-done.3 = bf16[2,2,2,4,4096]{4,3,2,1,0:T(4,128)(2,1)S(1)} collective-permute-done((bf16[2,2,2,4,4096]{4,3,2,1,0:T(4,128)(2,1)S(1)}, bf16[2,2,2,4,4096]{4,3,2,1,0:T(4,128)(2,1)S(1)}, u32[]{:S(2)}, u32[]{:S(2)}) %collective-permute-start.3) | collective-permute-done | bytes 262176 | tf_op jit(solution)/shard_map/ppermute | solution.py:18
  36.7 4.7 %copy.425 = bf16[4096,3,128]{0,2,1:T(8,128)(2,1)} copy(bf16[4096,3,128]{2,0,1:T(8,128)(2,1)} %param.17) | data formatting | bytes 6291456 | tf_op args[3]
  42.6 2.0 gather_fusion
  46.6 1.7 select_bitcast_fusion.1
  49.0 2.1 copy.424
  51.1 1.5 dot_general.32
  52.5 3.0 %fusion.112 = f32[4,32,384]{2,1,0:T(8,128)S(1)} fusion(bf16[4,32,4096]{2,1,0:T(8,128)(2,1)S(1)} %dot_general.32, bf16[4096,384,1]{0,1,2:T(8,128)(2,1)} %bitcast.264), kind=kOutput, calls=%fused_computation.219 | convolution fusion | flops 402653184 | bytes 4390912 | tf_op jit(solution)/shard_map/dot_general | solution.py:118
  58.8 1.6 copy.483
  66.3 13.3 %all_gather.3 = bf16[4,8,32,128]{3,2,0,1:T(8,128)(2,1)S(1)} all-gather(bf16[4,1,32,128]{3,2,0,1:T(8,128)(2,1)} %copy.431), channel_id=1, replica_groups=mesh['batch'=8,'tensor'=32] {'batch'}, dimensions={1}, use_global_device_ids=true | all-gather | bytes 294912 | tf_op jit(solution)/shard_map/all_gather | solution.py:135
  82.6 1.8 collective-permute-start.6
  86.6 1.8 collective-permute-start.7
  88.4 3.5 %collective-permute-done.6 = f32[4,8,32,4]{1,3,0,2:T(4,128)S(1)} collective-permute-done((f32[4,8,32,4]{1,3,0,2:T(4,128)S(1)}, f32[4,8,32,4]{1,3,0,2:T(4,128)S(1)}, u32[]{:S(2)}, u32[]{:S(2)}) %collective-permute-start.6) | collective-permute-done | bytes 16416 | tf_op jit(solution)/shard_map/ppermute | solution.py:18
  92.6 10.5 %collective-permute-done.5 = f32[4,8,32,64]{3,1,0,2:T(8,128)S(1)} collective-permute-done((f32[4,8,32,64]{3,1,0,2:T(8,128)S(1)}, f32[4,8,32,64]{3,1,0,2:T(8,128)S(1)}, u32[]{:S(2)}, u32[]{:S(2)}) %collective-permute-start.5) | collective-permute-done | bytes 262176 | tf_op jit(solution)/shard_map/ppermute | solution.py:18
  103.6 4.5 %collective-permute-done.7 = f32[4,8,4,512]{3,1,0,2:T(8,128)S(1)} collective-permute-done((f32[4,8,4,512]{3,1,0,2:T(8,128)S(1)}, f32[4,8,4,512]{3,1,0,2:T(8,128)S(1)}, u32[]{:S(2)}, u32[]{:S(2)}) %collective-permute-start.7) | collective-permute-done | bytes 262176 | tf_op jit(solution)/shard_map/ppermute | solution.py:18
  113.2 1.7 fusion.18
  115.6 1.5 copy.455
  117.1 1.7 fusion.26
  121.7 1.5 broadcast_in_dim.265
  124.6 1.5 broadcast_in_dim.262
  127.5 2.0 copy.458
  129.5 2.0 copy.459
  134.1 1.9 convolution_bitcast_fusion.1
  137.4 1.4 copy.460
  138.8 4.9 %all-to-all-start = ((f32[4,8,32,130]{3,0,2,1:T(4,128)}), f32[4,8,32,130]{3,0,2,1:T(4,128)}, u32[]{:S(2)}, u32[]{:S(2)}) async-start(f32[4,8,32,130]{3,0,2,1:T(4,128)} %copy.460), calls=%async_computation | async-start | bytes 2097152 | tf_op jit(solution)/shard_map/all_to_all | solution.py:232
  143.8 14.6 %all-to-all-done = f32[4,8,32,130]{3,0,2,1:T(4,128)} async-done(((f32[4,8,32,130]{3,0,2,1:T(4,128)}), f32[4,8,32,130]{3,0,2,1:T(4,128)}, u32[]{:S(2)}, u32[]{:S(2)}) %all-to-all-start) | async-done | bytes 532512 | tf_op jit(solution)/shard_map/all_to_all | solution.py:232
  158.4 2.6 %fusion.107 = (f32[4,8,32,1]{3,0,2,1:T(4,128)}, f32[4,32]{0,1:T(8,128)S(1)}, f32[4,8,32,1]{3,0,2,1:T(4,128)}) fusion(f32[4,8,32,130]{3,0,2,1:T(4,128)} %all-to-all-done), kind=kLoop, calls=%fused_computation.214 | loop fusion | flops 896 | bytes 16896 | tf_op jit(solution)/shard_map/slice | solution.py:235
  165.5 2.9 %fusion.10 = f32[4,32,4096]{2,1,0:T(8,128)} fusion(bf16[128,4096]{1,0:T(8,128)(2,1)} %param.18, bf16[4,32,128]{2,0,1:T(4,128)(2,1)S(1)} %divide_convert_fusion), kind=kOutput, calls=%fused_computation.19 | convolution fusion | flops 134217728 | bytes 3178496 | tf_op jit(solution)/shard_map/src,cd->rsd/dot_general | solution.py:242
  168.4 4.9 %fusion = f32[32,4,4096]{2,0,1:T(8,128)} fusion(f32[4,32,4096]{2,1,0:T(8,128)} %fusion.10, bf16[256,4096]{1,0:T(8,128)(2,1)S(1)} %copy-done, bf16[4,32,4096]{2,1,0:T(8,128)(2,1)S(1)} %dot_general.32, bf16[4096,256]{1,0:T(8,128)(2,1)} %param.19, f32[256]{0:T(256)S(1)} %copy-done.23), kind=kOutput, calls=%fused_computation.2 | convolution fusion | flops 537722880 | bytes 9438208 | tf_op jit(solution)/shard_map/srf,fd->rsd/dot_general | solution.py:244
  173.3 3.5 %reshape.474 = f32[2,2,2,2,2,4,4096]{6,4,3,2,1,0,5:T(2,128)} reshape(f32[32,4,4096]{2,0,1:T(8,128)} %fusion) | data formatting | bytes 4194304 | tf_op jit(solution)/shard_map/reshape | solution.py:25
  176.8 4.4 %constant_dynamic-slice_fusion.1 = (f32[2,2,2,2,1,4,4096]{6,4,3,2,1,0,5:T(1,128)S(1)}, f32[2,2,2,2,1,4,4096]{6,4,3,2,1,0,5:T(1,128)S(1)}) fusion(f32[2,2,2,2,2,4,4096]{6,4,3,2,1,0,5:T(2,128)} %reshape.474, s32[]{:T(128)S(6)} %select_n.266, s32[]{:T(128)S(6)} %select_n.267), kind=kLoop, calls=%fused_computation.188 | loop fusion | bytes 4194312 | tf_op jit(solution)/shard_map/jit(dynamic_index_in_dim)/dynamic_slice | solution.py:30
  181.2 1.7 copy.508
  182.9 1.7 collective-permute-start.8
  184.6 23.2 %collective-permute-done.8 = f32[2,2,2,2,4,4096]{5,4,3,2,0,1:T(4,128)} collective-permute-done((f32[2,2,2,2,4,4096]{5,4,3,2,0,1:T(4,128)}, f32[2,2,2,2,4,4096]{5,4,3,2,0,1:T(4,128)}, u32[]{:S(2)}, u32[]{:S(2)}) %collective-permute-start.8) | collective-permute-done | bytes 1048608 | tf_op jit(solution)/shard_map/ppermute | solution.py:18
  207.9 2.1 bitcast_add_fusion
  211.0 1.7 collective-permute-start.9
  212.7 10.9 %collective-permute-done.9 = f32[2,2,2,4,4096]{4,3,2,1,0:T(4,128)S(1)} collective-permute-done((f32[2,2,2,4,4096]{4,3,2,1,0:T(4,128)S(1)}, f32[2,2,2,4,4096]{4,3,2,1,0:T(4,128)S(1)}, u32[]{:S(2)}, u32[]{:S(2)}) %collective-permute-start.9) | collective-permute-done | bytes 524320 | tf_op jit(solution)/shard_map/ppermute | solution.py:18
  224.8 2.8 %collective-permute-start.10 = (f32[2,2,4,4096]{3,2,1,0:T(4,128)S(1)}, f32[2,2,4,4096]{3,2,1,0:T(4,128)S(1)}, u32[]{:S(2)}, u32[]{:S(2)}) collective-permute-start(f32[2,2,4,4096]{3,2,1,0:T(4,128)S(1)} %dynamic-slice_bitcast_fusion.1), channel_id=1, source_target_pairs={{0,2},{1,3},{2,0},{3,1},{4,6},{5,7},{6,4},{7,5},{8,10},{9,11},{10,... | collective-permute-start | bytes 786440 | tf_op jit(solution)/shard_map/ppermute | solution.py:18
  227.6 9.9 %collective-permute-done.10 = f32[2,2,4,4096]{3,2,1,0:T(4,128)S(1)} collective-permute-done((f32[2,2,4,4096]{3,2,1,0:T(4,128)S(1)}, f32[2,2,4,4096]{3,2,1,0:T(4,128)S(1)}, u32[]{:S(2)}, u32[]{:S(2)}) %collective-permute-start.10) | collective-permute-done | bytes 262176 | tf_op jit(solution)/shard_map/ppermute | solution.py:18
  237.6 3.3 %collective-permute-start.11 = (f32[2,4,4096]{2,1,0:T(4,128)S(1)}, f32[2,4,4096]{2,1,0:T(4,128)S(1)}, u32[]{:S(2)}, u32[]{:S(2)}) collective-permute-start(f32[2,4,4096]{2,1,0:T(4,128)S(1)} %dynamic-slice_bitcast_fusion.2), channel_id=1, source_target_pairs={{0,16},{1,17},{2,18},{3,19},{4,20},{5,21},{6,22},{7,23},{8,24},{9,... | collective-permute-start | bytes 393224 | tf_op jit(solution)/shard_map/ppermute | solution.py:18
  240.9 3.3 %collective-permute-done.11 = f32[2,4,4096]{2,1,0:T(4,128)S(1)} collective-permute-done((f32[2,4,4096]{2,1,0:T(4,128)S(1)}, f32[2,4,4096]{2,1,0:T(4,128)S(1)}, u32[]{:S(2)}, u32[]{:S(2)}) %collective-permute-start.11) | collective-permute-done | bytes 131104 | tf_op jit(solution)/shard_map/ppermute | solution.py:18
  244.2 5.4 %collective-permute-start.12 = (f32[4,4096]{1,0:T(4,128)S(1)}, f32[4,4096]{1,0:T(4,128)S(1)}, u32[]{:S(2)}, u32[]{:S(2)}) collective-permute-start(f32[4,4096]{1,0:T(4,128)S(1)} %dynamic-slice_bitcast_fusion.3), channel_id=1, source_target_pairs={{0,4},{1,5},{2,6},{3,7},{4,0},{5,1},{6,2},{7,3},{8,12},{9,13},{10,... | collective-permute-start | bytes 196616 | tf_op jit(solution)/shard_map/ppermute | solution.py:18
  249.6 2.9 %collective-permute-done.12 = f32[4,4096]{1,0:T(4,128)S(1)} collective-permute-done((f32[4,4096]{1,0:T(4,128)S(1)}, f32[4,4096]{1,0:T(4,128)S(1)}, u32[]{:S(2)}, u32[]{:S(2)}) %collective-permute-start.12) | collective-permute-done | bytes 65568 | tf_op jit(solution)/shard_map/ppermute | solution.py:18
  (157 shorter events, 52.9 us)
Async XLA Ops:
  0.0 168.4 %copy-start = (bf16[256,4096]{1,0:T(8,128)(2,1)S(1)}, bf16[256,4096]{1,0:T(8,128)(2,1)}, u32[]{:S(2)}) copy-start(bf16[256,4096]{1,0:T(8,128)(2,1)} %param.21) | copy-start | bytes 6291460
  2.9 9.5 %collective-permute-start = (bf16[4,4096]{1,0:T(4,128)(2,1)S(1)}, bf16[4,4096]{1,0:T(4,128)(2,1)S(1)}, u32[]{:S(2)}, u32[]{:S(2)}) collective-permute-start(bf16[4,4096]{1,0:T(4,128)(2,1)S(1)} %fusion.65), channel_id=1, source_target_pairs={{0,4},{1,5},{2,6},{3,7},{4,0},{5,1},{6,2},{7,3},{8,12},{9,13},{10,... | collective-permute-start | bytes 98312 | tf_op jit(solution)/shard_map/ppermute | solution.py:18
  12.0 24.6 %copy-start.24 = (s32[32]{0:T(128)S(1)}, s32[32]{0:T(128)}, u32[]{:S(2)}) copy-start(s32[32]{0:T(128)} %param.26) | copy-start | bytes 388
  13.4 5.9 %collective-permute-start.1 = (bf16[2,4,4096]{2,1,0:T(4,128)(2,1)S(1)}, bf16[2,4,4096]{2,1,0:T(4,128)(2,1)S(1)}, u32[]{:S(2)}, u32[]{:S(2)}) collective-permute-start(bf16[2,4,4096]{2,1,0:T(4,128)(2,1)S(1)} %pad_maximum_fusion.4), channel_id=1, source_target_pairs={{0,16},{1,17},{2,18},{3,19},{4,20},{5,21},{6,22},{7,23},{8,24},{9,... | collective-permute-start | bytes 196616 | tf_op jit(solution)/shard_map/ppermute | solution.py:18
  19.4 7.6 %collective-permute-start.2 = (bf16[2,2,4,4096]{3,2,1,0:T(4,128)(2,1)S(1)}, bf16[2,2,4,4096]{3,2,1,0:T(4,128)(2,1)S(1)}, u32[]{:S(2)}, u32[]{:S(2)}) collective-permute-start(bf16[2,2,4,4096]{3,2,1,0:T(4,128)(2,1)S(1)} %pad_maximum_fusion.3), channel_id=1, source_target_pairs={{0,2},{1,3},{2,0},{3,1},{4,6},{5,7},{6,4},{7,5},{8,10},{9,11},{10,... | collective-permute-start | bytes 393224 | tf_op jit(solution)/shard_map/ppermute | solution.py:18
  27.4 6.5 %collective-permute-start.3 = (bf16[2,2,2,4,4096]{4,3,2,1,0:T(4,128)(2,1)S(1)}, bf16[2,2,2,4,4096]{4,3,2,1,0:T(4,128)(2,1)S(1)}, u32[]{:S(2)}, u32[]{:S(2)}) collective-permute-start(bf16[2,2,2,4,4096]{4,3,2,1,0:T(4,128)(2,1)S(1)} %pad_maximum_fusion.2), channel_id=1, source_target_pairs={{0,8},{1,9},{2,10},{3,11},{4,12},{5,13},{6,14},{7,15},{8,0},{9,1},... | collective-permute-start | bytes 786440 | tf_op jit(solution)/shard_map/ppermute | solution.py:18
  34.1 0.7 copy-start.6
  36.0 10.6 %collective-permute-start.4 = (bf16[2,2,2,2,4,4096]{5,4,3,2,1,0:T(4,128)(2,1)}, bf16[2,2,2,2,4,4096]{5,4,3,2,1,0:T(4,128)(2,1)}, u32[]{:S(2)}, u32[]{:S(2)}) collective-permute-start(bf16[2,2,2,2,4,4096]{5,4,3,2,1,0:T(4,128)(2,1)} %pad_maximum_fusion.1), channel_id=1, source_target_pairs={{0,1},{1,0},{2,3},{3,2},{4,5},{5,4},{6,7},{7,6},{8,9},{9,8},{10,11... | collective-permute-start | bytes 1572872 | tf_op jit(solution)/shard_map/ppermute | solution.py:18
  41.7 61.4 %copy-start.15 = (pred[4,8,32]{1,0,2:T(4,128)(4,1)}, pred[4,8,32]{1,0,2:T(4,128)(4,1)S(1)}, u32[]{:S(2)}) copy-start(pred[4,8,32]{1,0,2:T(4,128)(4,1)S(1)} %copy.423) | copy-start | bytes 3076
  44.5 2.0 copy-start.7
  81.3 5.0 %copy-start.11 = (bf16[4,4,1,128,128]{4,3,2,1,0:T(8,128)(2,1)S(1)}, bf16[4,4,1,128,128]{4,3,2,1,0:T(8,128)(2,1)}, u32[]{:S(2)}) copy-start(bf16[4,4,1,128,128]{4,3,2,1,0:T(8,128)(2,1)} %get-tuple-element.22) | copy-start | bytes 1572868
  82.6 9.3 %copy-start.4 = (f32[4,8,32,4]{1,3,0,2:T(4,128)}, f32[4,8,32,4]{1,3,0,2:T(4,128)S(1)}, u32[]{:S(2)}) copy-start(f32[4,8,32,4]{1,3,0,2:T(4,128)S(1)} %convolution_bitcast_fusion.4) | copy-start | bytes 49156
  82.6 26.2 %copy-start.17 = (pred[4,512]{1,0:T(4,128)(4,1)S(1)}, pred[4,512]{1,0:T(4,128)(4,1)}, u32[]{:S(2)}) copy-start(pred[4,512]{1,0:T(4,128)(4,1)} %iota_compare_fusion.7) | copy-start | bytes 6148
  82.6 26.3 %copy-start.21 = (pred[32]{0:T(512)(128)(4,1)S(1)}, pred[32]{0:T(512)(128)(4,1)}, u32[]{:S(2)}) copy-start(pred[32]{0:T(512)(128)(4,1)} %broadcast_in_dim.249) | copy-start | bytes 100
  82.6 9.3 %collective-permute-start.6 = (f32[4,8,32,4]{1,3,0,2:T(4,128)S(1)}, f32[4,8,32,4]{1,3,0,2:T(4,128)S(1)}, u32[]{:S(2)}, u32[]{:S(2)}) collective-permute-start(f32[4,8,32,4]{1,3,0,2:T(4,128)S(1)} %convolution_bitcast_fusion.4), channel_id=1, source_target_pairs={{0,1},{1,0},{2,3},{3,2},{4,5},{5,4},{6,7},{7,6},{8,9},{9,8},{10,11... | collective-permute-start | bytes 49160 | tf_op jit(solution)/shard_map/ppermute | solution.py:18
  85.8 17.3 %copy-start.1 = (f32[4,8,32,64]{3,1,0,2:T(8,128)}, f32[4,8,32,64]{3,1,0,2:T(8,128)S(1)}, u32[]{:S(2)}) copy-start(f32[4,8,32,64]{3,1,0,2:T(8,128)S(1)} %convolution_bitcast_fusion.2) | copy-start | bytes 786436
  85.8 17.3 %collective-permute-start.5 = (f32[4,8,32,64]{3,1,0,2:T(8,128)S(1)}, f32[4,8,32,64]{3,1,0,2:T(8,128)S(1)}, u32[]{:S(2)}, u32[]{:S(2)}) collective-permute-start(f32[4,8,32,64]{3,1,0,2:T(8,128)S(1)} %convolution_bitcast_fusion.2), channel_id=1, source_target_pairs={{0,1},{1,0},{2,3},{3,2},{4,5},{5,4},{6,7},{7,6},{8,9},{9,8},{10,11... | collective-permute-start | bytes 786440 | tf_op jit(solution)/shard_map/ppermute | solution.py:18
  86.6 21.5 %collective-permute-start.7 = (f32[4,8,4,512]{3,1,0,2:T(8,128)S(1)}, f32[4,8,4,512]{3,1,0,2:T(8,128)S(1)}, u32[]{:S(2)}, u32[]{:S(2)}) collective-permute-start(f32[4,8,4,512]{3,1,0,2:T(8,128)S(1)} %convolution_bitcast_fusion.3), channel_id=1, source_target_pairs={{0,1},{1,0},{2,3},{3,2},{4,5},{5,4},{6,7},{7,6},{8,9},{9,8},{10,11... | collective-permute-start | bytes 786440 | tf_op jit(solution)/shard_map/ppermute | solution.py:18
  91.9 0.7 copy-start.12
  103.1 5.8 %copy-start.10 = (f32[4,8,32,64]{3,1,0,2:T(8,128)}, f32[4,8,32,64]{3,1,0,2:T(8,128)S(1)}, u32[]{:S(2)}) copy-start(f32[4,8,32,64]{3,1,0,2:T(8,128)S(1)} %collective-permute-done.5) | copy-start | bytes 786436
  103.6 22.6 %copy-start.22 = (pred[32]{0:T(512)(128)(4,1)S(1)}, pred[32]{0:T(512)(128)(4,1)}, u32[]{:S(2)}) copy-start(pred[32]{0:T(512)(128)(4,1)} %broadcast_in_dim.249) | copy-start | bytes 100
  108.1 0.7 copy-start.3
  111.8 19.7 %copy-start.18 = (pred[4,512]{1,0:T(4,128)(4,1)S(1)}, pred[4,512]{1,0:T(4,128)(4,1)}, u32[]{:S(2)}) copy-start(pred[4,512]{1,0:T(4,128)(4,1)} %iota_compare_fusion.7) | copy-start | bytes 6148
  134.0 1.9 copy-start.5
  134.0 1.9 copy-start.13
  134.0 1.9 copy-start.16
  134.0 1.9 copy-start.19
  135.9 1.0 copy-start.8
  135.9 1.2 copy-start.9
  138.8 19.6 %all-to-all-start = ((f32[4,8,32,130]{3,0,2,1:T(4,128)}), f32[4,8,32,130]{3,0,2,1:T(4,128)}, u32[]{:S(2)}, u32[]{:S(2)}) async-start(f32[4,8,32,130]{3,0,2,1:T(4,128)} %copy.460), calls=%async_computation | async-start | bytes 2097152 | tf_op jit(solution)/shard_map/all_to_all | solution.py:232
  163.7 4.7 %copy-start.23 = (f32[256]{0:T(256)S(1)}, f32[256]{0:T(256)}, u32[]{:S(2)}) copy-start(f32[256]{0:T(256)} %param.20) | copy-start | bytes 3076
  182.9 24.9 %collective-permute-start.8 = (f32[2,2,2,2,4,4096]{5,4,3,2,0,1:T(4,128)}, f32[2,2,2,2,4,4096]{5,4,3,2,0,1:T(4,128)}, u32[]{:S(2)}, u32[]{:S(2)}) collective-permute-start(f32[2,2,2,2,4,4096]{5,4,3,2,0,1:T(4,128)} %bitcast.263), channel_id=1, source_target_pairs={{0,1},{1,0},{2,3},{3,2},{4,5},{5,4},{6,7},{7,6},{8,9},{9,8},{10,11... | collective-permute-start | bytes 3145736 | tf_op jit(solution)/shard_map/ppermute | solution.py:18
  209.9 1.0 copy-start.2
  211.0 41.5 %copy-start.14 = (bf16[4,1,1,4096]{3,0,2,1:T(4,128)(2,1)S(1)}, bf16[4,1,1,4096]{3,0,2,1:T(4,128)(2,1)}, u32[]{:S(2)}) copy-start(bf16[4,1,1,4096]{3,0,2,1:T(4,128)(2,1)} %param.14) | copy-start | bytes 98308
  211.0 41.5 %copy-start.20 = (f32[4096]{0:T(1024)S(1)}, f32[4096]{0:T(1024)}, u32[]{:S(2)}) copy-start(f32[4096]{0:T(1024)} %param.22) | copy-start | bytes 49156
  211.0 12.6 %collective-permute-start.9 = (f32[2,2,2,4,4096]{4,3,2,1,0:T(4,128)S(1)}, f32[2,2,2,4,4096]{4,3,2,1,0:T(4,128)S(1)}, u32[]{:S(2)}, u32[]{:S(2)}) collective-permute-start(f32[2,2,2,4,4096]{4,3,2,1,0:T(4,128)S(1)} %dynamic-slice_bitcast_fusion), channel_id=1, source_target_pairs={{0,8},{1,9},{2,10},{3,11},{4,12},{5,13},{6,14},{7,15},{8,0},{9,1},... | collective-permute-start | bytes 1572872 | tf_op jit(solution)/shard_map/ppermute | solution.py:18
  224.8 12.7 %collective-permute-start.10 = (f32[2,2,4,4096]{3,2,1,0:T(4,128)S(1)}, f32[2,2,4,4096]{3,2,1,0:T(4,128)S(1)}, u32[]{:S(2)}, u32[]{:S(2)}) collective-permute-start(f32[2,2,4,4096]{3,2,1,0:T(4,128)S(1)} %dynamic-slice_bitcast_fusion.1), channel_id=1, source_target_pairs={{0,2},{1,3},{2,0},{3,1},{4,6},{5,7},{6,4},{7,5},{8,10},{9,11},{10,... | collective-permute-start | bytes 786440 | tf_op jit(solution)/shard_map/ppermute | solution.py:18
  237.6 6.6 %collective-permute-start.11 = (f32[2,4,4096]{2,1,0:T(4,128)S(1)}, f32[2,4,4096]{2,1,0:T(4,128)S(1)}, u32[]{:S(2)}, u32[]{:S(2)}) collective-permute-start(f32[2,4,4096]{2,1,0:T(4,128)S(1)} %dynamic-slice_bitcast_fusion.2), channel_id=1, source_target_pairs={{0,16},{1,17},{2,18},{3,19},{4,20},{5,21},{6,22},{7,23},{8,24},{9,... | collective-permute-start | bytes 393224 | tf_op jit(solution)/shard_map/ppermute | solution.py:18
  244.2 8.3 %collective-permute-start.12 = (f32[4,4096]{1,0:T(4,128)S(1)}, f32[4,4096]{1,0:T(4,128)S(1)}, u32[]{:S(2)}, u32[]{:S(2)}) collective-permute-start(f32[4,4096]{1,0:T(4,128)S(1)} %dynamic-slice_bitcast_fusion.3), channel_id=1, source_target_pairs={{0,4},{1,5},{2,6},{3,7},{4,0},{5,1},{6,2},{7,3},{8,12},{9,13},{10,... | collective-permute-start | bytes 196616 | tf_op jit(solution)/shard_map/ppermute | solution.py:18

commit v3 on v2

--- a/solution.py
+++ b/solution.py
@@ -10,8 +10,8 @@
 BEAMS = 8
 
 NEG_FILL = -1e30
-SCATTER_ORDER = (0, 3, 1, 4, 2)
-GATHER_ORDER = (2, 4, 1, 3, 0)
+SCATTER_ORDERS = ((0, 3, 1, 4, 2), (3, 0, 4, 1, 2))
+GATHER_ORDERS = ((2, 4, 1, 3, 0), (2, 1, 4, 0, 3))
 
 
 def partner(value, axis, bit):
@@ -51,6 +51,11 @@
     perm = rest[:out_axis] + lead + rest[out_axis:]
     x = jnp.transpose(x, perm)
     return x.reshape(x.shape[:out_axis] + (n,) + x.shape[out_axis + nbits :])
+
+
+def split_last(x, count):
+    width = x.shape[-1] // count
+    return [x[..., i * width : (i + 1) * width] for i in range(count)]
 
 
 def normalize(row_block, norm_gain, norm_bias):
@@ -112,7 +117,13 @@
     first_column = tensor_index * columns
 
     normed = normalize(inputs[:, 0], norm_gain, norm_bias).astype(jnp.bfloat16)
-    rows = tree_all_gather(normed[:, 0], "tensor", GATHER_ORDER, 1)
+    rows = jnp.concatenate(
+        [
+            tree_all_gather(piece, "tensor", order, 1)
+            for piece, order in zip(split_last(normed[:, 0], len(GATHER_ORDERS)), GATHER_ORDERS)
+        ],
+        axis=-1,
+    )
     flat = rows.reshape(steps * requests, model_width)
     qkv_flat = qkv_weight.reshape(model_width, 3 * columns)
     projected = jnp.dot(flat, qkv_flat, preferred_element_type=jnp.float32).reshape(
@@ -242,7 +253,13 @@
     update = jnp.einsum(
         "src,cd->rsd", attention, out_weight, preferred_element_type=jnp.float32
     ) + jnp.einsum("srf,fd->rsd", hidden, down_weight, preferred_element_type=jnp.float32)
-    summed = tree_reduce_scatter(update, "tensor", SCATTER_ORDER)
+    summed = jnp.concatenate(
+        [
+            tree_reduce_scatter(piece, "tensor", order)
+            for piece, order in zip(split_last(update, len(SCATTER_ORDERS)), SCATTER_ORDERS)
+        ],
+        axis=-1,
+    )
     result = inputs[:, 0].astype(jnp.float32) + summed[:, None] + down_bias
     return result[:, None]
 

time: 256 us -> 226 us (0.88)
  waiting for transfers between devices: 95.5 us -> 75.9 us
  local copies, waits for them, and re-layouts: 58.2 us -> 47.5 us
  starting transfers between devices: 37.8 us -> 42.8 us
  other arithmetic: 30.4 us -> 25.8 us
    ppermute x13 -> x23, waiting for transfers between devices: 80.9 us -> 61.5 us  [partner(): lax.ppermute(value, axis, [(i, i ^ 1 << bit) for i in range(lax.axis_size...]
    ppermute x13 -> x23, starting transfers between devices: 32.9 us -> 38.3 us  [partner(): lax.ppermute(value, axis, [(i, i ^ 1 << bit) for i in range(lax.axis_size...]
    unnamed x59 -> x52, local copies, waits for them, and re-layouts: 15.6 us -> 10.4 us
    slice x0 -> x2, local copies, waits for them, and re-layouts: none -> 3.11 us  [split_last(): return [x[..., i * width:(i + 1) * width] for i in range(count)]]
  transfers between devices with their start and end apart: 14 -> 24, of which waited for: 13 -> 20; matrix products, arithmetic and copies ran while one was open for 6% -> 11% of each run, Pallas kernels for 0% -> 0%
where the time goes in v3:
time: 226 us; the launch traced here: 225 us
  waiting for transfers between devices  75.9 us (34%)
  local copies, waits for them, and re-layouts  47.5 us (21%)
  starting transfers between devices  42.8 us (19%)
  other arithmetic  25.8 us (11%)
  matrix products  18.8 us (8%)
  blocking collectives  12.9 us (6%)
    ppermute x23, waiting for transfers between devices, partner(): lax.ppermute(value, axis, [(i, i ^ 1 << bit) for i in range(lax.axis_size...  61.5 us
    ppermute x23, starting transfers between devices, partner(): lax.ppermute(value, axis, [(i, i ^ 1 << bit) for i in range(lax.axis_size...  38.3 us
    all_to_all x1, waiting for transfers between devices, on_device(): received = lax.all_to_all(packed, 'batch', 1, 1, tiled=True)  14.5 us
    all_gather x1, blocking collectives, on_device(): query_all = lax.all_gather(queries[:, None], 'batch', axis=1, tiled=True)  12.9 us
    unnamed x52, local copies, waits for them, and re-layouts  10.4 us
    broadcast_in_dim x6, local copies, waits for them, and re-layouts, spread(): placed = jnp.where(slot_hit, values[..., None], fill)  6.57 us
    dot_general x1, matrix products, on_device(): jnp.einsum('srf,fd->rsd', hidden, down_weight, preferred_element_type=jnp...  4.9 us
  transfers between devices with their start and end apart: 24, of which 20 were waited for; matrix products, arithmetic and copies ran while one was open for 11% of the time, Pallas kernels for 0%

profile of v3, /device:TPU:2, one launch (start us, length us, event | category | flops | bytes accessed | tf_op | source)
XLA Modules:
  0.0 224.6 jit_solution(14965270586914968104)
XLA Ops:
  3.8 7.3 %collective-permute-start.5 = (bf16[4,2048]{1,0:T(4,128)(2,1)S(1)}, bf16[4,2048]{1,0:T(4,128)(2,1)S(1)}, u32[]{:S(2)}, u32[]{:S(2)}) collective-permute-start(bf16[4,2048]{1,0:T(4,128)(2,1)S(1)} %slice.98), channel_id=1, source_target_pairs={{0,4},{1,5},{2,6},{3,7},{4,0},{5,1},{6,2},{7,3},{8,12},{9,13},{10,... | collective-permute-start | bytes 49160 | tf_op jit(solution)/shard_map/ppermute | solution.py:18
  15.1 2.0 gather_fusion
  19.7 4.7 %copy.465 = bf16[4096,3,128]{0,2,1:T(8,128)(2,1)} copy(bf16[4096,3,128]{2,0,1:T(8,128)(2,1)} %param.17) | data formatting | bytes 6291456 | tf_op args[3]
  25.5 2.1 collective-permute-start.6
  27.6 5.7 %collective-permute-done = bf16[4,2048]{1,0:T(4,128)(2,1)S(1)} collective-permute-done((bf16[4,2048]{1,0:T(4,128)(2,1)S(1)}, bf16[4,2048]{1,0:T(4,128)(2,1)S(1)}, u32[]{:S(2)}, u32[]{:S(2)}) %collective-permute-start) | collective-permute-done | bytes 16416 | tf_op jit(solution)/shard_map/ppermute | solution.py:18
  33.4 3.3 %collective-permute-start.1 = (bf16[2,4,2048]{2,1,0:T(4,128)(2,1)S(1)}, bf16[2,4,2048]{2,1,0:T(4,128)(2,1)S(1)}, u32[]{:S(2)}, u32[]{:S(2)}) collective-permute-start(bf16[2,4,2048]{2,1,0:T(4,128)(2,1)S(1)} %pad_maximum_fusion.9), channel_id=1, source_target_pairs={{0,16},{1,17},{2,18},{3,19},{4,20},{5,21},{6,22},{7,23},{8,24},{9,... | collective-permute-start | bytes 98312 | tf_op jit(solution)/shard_map/ppermute | solution.py:18
  37.2 1.7 collective-permute-done.1
  40.3 2.3 %collective-permute-done.7 = bf16[2,2,4,2048]{3,2,1,0:T(4,128)(2,1)S(1)} collective-permute-done((bf16[2,2,4,2048]{3,2,1,0:T(4,128)(2,1)S(1)}, bf16[2,2,4,2048]{3,2,1,0:T(4,128)(2,1)S(1)}, u32[]{:S(2)}, u32[]{:S(2)}) %collective-permute-start.7) | collective-permute-done | bytes 65568 | tf_op jit(solution)/shard_map/ppermute | solution.py:18
  44.8 1.6 collective-permute-start.3
  46.4 1.4 collective-permute-done.8
  48.9 2.3 %collective-permute-done.3 = bf16[2,2,2,4,2048]{4,3,2,1,0:T(4,128)(2,1)S(1)} collective-permute-done((bf16[2,2,2,4,2048]{4,3,2,1,0:T(4,128)(2,1)S(1)}, bf16[2,2,2,4,2048]{4,3,2,1,0:T(4,128)(2,1)S(1)}, u32[]{:S(2)}, u32[]{:S(2)}) %collective-permute-start.3) | collective-permute-done | bytes 131104 | tf_op jit(solution)/shard_map/ppermute | solution.py:18
  56.1 2.9 %collective-permute-done.4 = bf16[2,2,2,2,4,2048]{5,4,3,2,1,0:T(4,128)(2,1)} collective-permute-done((bf16[2,2,2,2,4,2048]{5,4,3,2,1,0:T(4,128)(2,1)}, bf16[2,2,2,2,4,2048]{5,4,3,2,1,0:T(4,128)(2,1)}, u32[]{:S(2)}, u32[]{:S(2)}) %collective-permute-start.4) | collective-permute-done | bytes 262176 | tf_op jit(solution)/shard_map/ppermute | solution.py:18
  63.3 3.3 %fusion.111 = f32[4,32,384]{2,1,0:T(8,128)S(1)} fusion(bf16[4,32,4096]{2,1,0:T(8,128)(2,1)S(1)} %constant_dynamic-update-slice_fusion, bf16[4096,384,1]{0,1,2:T(8,128)(2,1)} %bitcast.297), kind=kOutput, calls=%fused_computation.248 | convolution fusion | flops 402653184 | bytes 4390912 | tf_op jit(solution)/shard_map/dot_general | solution.py:129
  69.1 12.9 %all_gather.3 = bf16[4,8,32,128]{3,2,0,1:T(8,128)(2,1)S(1)} all-gather(bf16[4,1,32,128]{3,2,0,1:T(8,128)(2,1)S(1)} %copy.471), channel_id=1, replica_groups=mesh['batch'=8,'tensor'=32] {'batch'}, dimensions={1}, use_global_device_ids=true | all-gather | bytes 294912 | tf_op jit(solution)/shard_map/all_gather | solution.py:146
  84.7 1.4 convolution_bitcast_fusion.2
  89.9 2.8 %collective-permute-done.11 = f32[4,8,32,4]{1,3,0,2:T(4,128)S(1)} collective-permute-done((f32[4,8,32,4]{1,3,0,2:T(4,128)S(1)}, f32[4,8,32,4]{1,3,0,2:T(4,128)S(1)}, u32[]{:S(2)}, u32[]{:S(2)}) %collective-permute-start.11) | collective-permute-done | bytes 16416 | tf_op jit(solution)/shard_map/ppermute | solution.py:18
  93.7 10.2 %collective-permute-done.10 = f32[4,8,32,64]{3,1,0,2:T(8,128)S(1)} collective-permute-done((f32[4,8,32,64]{3,1,0,2:T(8,128)S(1)}, f32[4,8,32,64]{3,1,0,2:T(8,128)S(1)}, u32[]{:S(2)}, u32[]{:S(2)}) %collective-permute-start.10) | collective-permute-done | bytes 262176 | tf_op jit(solution)/shard_map/ppermute | solution.py:18
  104.4 4.5 %collective-permute-done.12 = f32[4,8,4,512]{3,1,0,2:T(8,128)S(1)} collective-permute-done((f32[4,8,4,512]{3,1,0,2:T(8,128)S(1)}, f32[4,8,4,512]{3,1,0,2:T(8,128)S(1)}, u32[]{:S(2)}, u32[]{:S(2)}) %collective-permute-start.12) | collective-permute-done | bytes 262176 | tf_op jit(solution)/shard_map/ppermute | solution.py:18
  113.2 1.6 fusion.18
  115.5 1.5 copy.495
  117.0 1.5 fusion.26
  119.8 1.4 broadcast_in_dim.262
  121.3 1.5 broadcast_in_dim.263
  122.8 1.4 broadcast_in_dim.251
  124.2 1.5 broadcast_in_dim.260
  127.2 2.0 copy.498
  129.2 2.0 copy.499
  133.6 1.7 convolution_bitcast_fusion.1
  138.1 4.5 %all-to-all-start = ((f32[4,8,32,130]{3,0,2,1:T(4,128)}), f32[4,8,32,130]{3,0,2,1:T(4,128)S(1)}, u32[]{:S(2)}, u32[]{:S(2)}) async-start(f32[4,8,32,130]{3,0,2,1:T(4,128)} %copy.500), calls=%async_computation | async-start | bytes 2097152 | tf_op jit(solution)/shard_map/all_to_all | solution.py:243
  142.6 14.5 %all-to-all-done = f32[4,8,32,130]{3,0,2,1:T(4,128)S(1)} async-done(((f32[4,8,32,130]{3,0,2,1:T(4,128)}), f32[4,8,32,130]{3,0,2,1:T(4,128)S(1)}, u32[]{:S(2)}, u32[]{:S(2)}) %all-to-all-start) | async-done | bytes 532512 | tf_op jit(solution)/shard_map/all_to_all | solution.py:243
  161.9 3.0 %fusion.10 = f32[4,32,4096]{2,1,0:T(8,128)} fusion(bf16[128,4096]{1,0:T(8,128)(2,1)} %param.18, bf16[4,32,128]{2,0,1:T(4,128)(2,1)S(1)} %divide_convert_fusion), kind=kOutput, calls=%fused_computation.17 | convolution fusion | flops 134217728 | bytes 3178496 | tf_op jit(solution)/shard_map/src,cd->rsd/dot_general | solution.py:253
  164.9 4.9 %fusion = f32[32,4,4096]{2,0,1:T(8,128)} fusion(f32[4,32,4096]{2,1,0:T(8,128)} %fusion.10, bf16[256,4096]{1,0:T(8,128)(2,1)S(1)} %copy-done, bf16[4,32,4096]{2,1,0:T(8,128)(2,1)S(1)} %copy-done.2, bf16[4096,256]{1,0:T(8,128)(2,1)} %param.19, f32[256]{0:T(256)S(1)} %copy-done.19), kind=kOutput, calls=%fused_computation.2 | convolution fusion | flops 537722880 | bytes 9438208 | tf_op jit(solution)/shard_map/srf,fd->rsd/dot_general | solution.py:255
  169.8 3.1 %fusion.105 = (f32[32,4,2048]{2,0,1:T(8,128)}, f32[32,4,2048]{2,0,1:T(8,128)}) fusion(f32[32,4,4096]{2,0,1:T(8,128)} %fusion), kind=kLoop, calls=%fused_computation.242 | loop fusion | bytes 4194304 | tf_op jit(solution)/shard_map/slice | solution.py:58
  172.9 1.8 reshape.499
  174.8 1.9 constant_dynamic-slice_fusion.3
  179.0 1.8 reshape.500
  182.5 9.1 %collective-permute-done.13 = f32[2,2,2,2,4,2048]{5,4,3,2,0,1:T(4,128)} collective-permute-done((f32[2,2,2,2,4,2048]{5,4,3,2,0,1:T(4,128)}, f32[2,2,2,2,4,2048]{5,4,3,2,0,1:T(4,128)}, u32[]{:S(2)}, u32[]{:S(2)}) %collective-permute-start.13) | collective-permute-done | bytes 524320 | tf_op jit(solution)/shard_map/ppermute | solution.py:18
  191.6 1.5 bitcast_add_fusion.1
  196.3 4.1 %collective-permute-done.14 = f32[2,2,2,4,2048]{4,3,2,1,0:T(4,128)S(1)} collective-permute-done((f32[2,2,2,4,2048]{4,3,2,1,0:T(4,128)S(1)}, f32[2,2,2,4,2048]{4,3,2,1,0:T(4,128)S(1)}, u32[]{:S(2)}, u32[]{:S(2)}) %collective-permute-start.14) | collective-permute-done | bytes 262176 | tf_op jit(solution)/shard_map/ppermute | solution.py:18
  200.5 1.6 collective-permute-start.15
  202.2 2.1 collective-permute-start.20
  204.3 3.6 %collective-permute-done.15 = f32[2,2,4,2048]{3,2,1,0:T(4,128)S(1)} collective-permute-done((f32[2,2,4,2048]{3,2,1,0:T(4,128)S(1)}, f32[2,2,4,2048]{3,2,1,0:T(4,128)S(1)}, u32[]{:S(2)}, u32[]{:S(2)}) %collective-permute-start.15) | collective-permute-done | bytes 131104 | tf_op jit(solution)/shard_map/ppermute | solution.py:18
  207.9 2.1 collective-permute-start.16
  210.0 1.5 collective-permute-start.21
  211.5 2.2 collective-permute-done.16
  215.9 4.1 %collective-permute-start.22 = (f32[4,2048]{1,0:T(4,128)S(1)}, f32[4,2048]{1,0:T(4,128)S(1)}, u32[]{:S(2)}, u32[]{:S(2)}) collective-permute-start(f32[4,2048]{1,0:T(4,128)S(1)} %dynamic-slice_bitcast_fusion.6), channel_id=1, source_target_pairs={{0,4},{1,5},{2,6},{3,7},{4,0},{5,1},{6,2},{7,3},{8,12},{9,13},{10,... | collective-permute-start | bytes 98312 | tf_op jit(solution)/shard_map/ppermute | solution.py:18
  220.0 1.8 collective-permute-done.17
  221.8 2.0 collective-permute-done.22
  (200 shorter events, 63.9 us)
Async XLA Ops:
  0.0 164.9 %copy-start = (bf16[256,4096]{1,0:T(8,128)(2,1)S(1)}, bf16[256,4096]{1,0:T(8,128)(2,1)}, u32[]{:S(2)}) copy-start(bf16[256,4096]{1,0:T(8,128)(2,1)} %param.21) | copy-start | bytes 6291460
  3.8 21.6 %collective-permute-start.5 = (bf16[4,2048]{1,0:T(4,128)(2,1)S(1)}, bf16[4,2048]{1,0:T(4,128)(2,1)S(1)}, u32[]{:S(2)}, u32[]{:S(2)}) collective-permute-start(bf16[4,2048]{1,0:T(4,128)(2,1)S(1)} %slice.98), channel_id=1, source_target_pairs={{0,4},{1,5},{2,6},{3,7},{4,0},{5,1},{6,2},{7,3},{8,12},{9,13},{10,... | collective-permute-start | bytes 49160 | tf_op jit(solution)/shard_map/ppermute | solution.py:18
  24.7 79.2 %copy-start.10 = (pred[4,8,32]{1,0,2:T(4,128)(4,1)}, pred[4,8,32]{1,0,2:T(4,128)(4,1)S(1)}, u32[]{:S(2)}) copy-start(pred[4,8,32]{1,0,2:T(4,128)(4,1)S(1)} %copy.462) | copy-start | bytes 3076
  25.4 7.9 %collective-permute-start = (bf16[4,2048]{1,0:T(4,128)(2,1)S(1)}, bf16[4,2048]{1,0:T(4,128)(2,1)S(1)}, u32[]{:S(2)}, u32[]{:S(2)}) collective-permute-start(bf16[4,2048]{1,0:T(4,128)(2,1)S(1)} %get-tuple-element.59), channel_id=1, source_target_pairs={{0,4},{1,5},{2,6},{3,7},{4,0},{5,1},{6,2},{7,3},{8,12},{9,13},{10,... | collective-permute-start | bytes 49160 | tf_op jit(solution)/shard_map/ppermute | solution.py:18
  25.5 11.1 %collective-permute-start.6 = (bf16[2,4,2048]{2,1,0:T(4,128)(2,1)S(1)}, bf16[2,4,2048]{2,1,0:T(4,128)(2,1)S(1)}, u32[]{:S(2)}, u32[]{:S(2)}) collective-permute-start(bf16[2,4,2048]{2,1,0:T(4,128)(2,1)S(1)} %pad_maximum_fusion.10), channel_id=1, source_target_pairs={{0,2},{1,3},{2,0},{3,1},{4,6},{5,7},{6,4},{7,5},{8,10},{9,11},{10,... | collective-permute-start | bytes 98312 | tf_op jit(solution)/shard_map/ppermute | solution.py:18
  33.4 5.5 %collective-permute-start.1 = (bf16[2,4,2048]{2,1,0:T(4,128)(2,1)S(1)}, bf16[2,4,2048]{2,1,0:T(4,128)(2,1)S(1)}, u32[]{:S(2)}, u32[]{:S(2)}) collective-permute-start(bf16[2,4,2048]{2,1,0:T(4,128)(2,1)S(1)} %pad_maximum_fusion.9), channel_id=1, source_target_pairs={{0,16},{1,17},{2,18},{3,19},{4,20},{5,21},{6,22},{7,23},{8,24},{9,... | collective-permute-start | bytes 98312 | tf_op jit(solution)/shard_map/ppermute | solution.py:18
  36.7 5.9 %collective-permute-start.7 = (bf16[2,2,4,2048]{3,2,1,0:T(4,128)(2,1)S(1)}, bf16[2,2,4,2048]{3,2,1,0:T(4,128)(2,1)S(1)}, u32[]{:S(2)}, u32[]{:S(2)}) collective-permute-start(bf16[2,2,4,2048]{3,2,1,0:T(4,128)(2,1)S(1)} %pad_maximum_fusion.6), channel_id=1, source_target_pairs={{0,16},{1,17},{2,18},{3,19},{4,20},{5,21},{6,22},{7,23},{8,24},{9,... | collective-permute-start | bytes 196616 | tf_op jit(solution)/shard_map/ppermute | solution.py:18
  39.0 5.7 %collective-permute-start.2 = (bf16[2,2,4,2048]{3,2,1,0:T(4,128)(2,1)S(1)}, bf16[2,2,4,2048]{3,2,1,0:T(4,128)(2,1)S(1)}, u32[]{:S(2)}, u32[]{:S(2)}) collective-permute-start(bf16[2,2,4,2048]{3,2,1,0:T(4,128)(2,1)S(1)} %pad_maximum_fusion.5), channel_id=1, source_target_pairs={{0,2},{1,3},{2,0},{3,1},{4,6},{5,7},{6,4},{7,5},{8,10},{9,11},{10,... | collective-permute-start | bytes 196616 | tf_op jit(solution)/shard_map/ppermute | solution.py:18
  42.8 5.1 %collective-permute-start.8 = (bf16[2,2,2,4,2048]{4,3,2,1,0:T(4,128)(2,1)S(1)}, bf16[2,2,2,4,2048]{4,3,2,1,0:T(4,128)(2,1)S(1)}, u32[]{:S(2)}, u32[]{:S(2)}) collective-permute-start(bf16[2,2,2,4,2048]{4,3,2,1,0:T(4,128)(2,1)S(1)} %pad_maximum_fusion.4), channel_id=1, source_target_pairs={{0,1},{1,0},{2,3},{3,2},{4,5},{5,4},{6,7},{7,6},{8,9},{9,8},{10,11... | collective-permute-start | bytes 393224 | tf_op jit(solution)/shard_map/ppermute | solution.py:18
  44.8 6.5 %collective-permute-start.3 = (bf16[2,2,2,4,2048]{4,3,2,1,0:T(4,128)(2,1)S(1)}, bf16[2,2,2,4,2048]{4,3,2,1,0:T(4,128)(2,1)S(1)}, u32[]{:S(2)}, u32[]{:S(2)}) collective-permute-start(bf16[2,2,2,4,2048]{4,3,2,1,0:T(4,128)(2,1)S(1)} %pad_maximum_fusion.3), channel_id=1, source_target_pairs={{0,8},{1,9},{2,10},{3,11},{4,12},{5,13},{6,14},{7,15},{8,0},{9,1},... | collective-permute-start | bytes 393224 | tf_op jit(solution)/shard_map/ppermute | solution.py:18
  48.2 6.5 %collective-permute-start.9 = (bf16[2,2,2,2,4,2048]{5,4,3,2,1,0:T(4,128)(2,1)S(1)}, bf16[2,2,2,2,4,2048]{5,4,3,2,1,0:T(4,128)(2,1)S(1)}, u32[]{:S(2)}, u32[]{:S(2)}) collective-permute-start(bf16[2,2,2,2,4,2048]{5,4,3,2,1,0:T(4,128)(2,1)S(1)} %pad_maximum_fusion.2), channel_id=1, source_target_pairs={{0,8},{1,9},{2,10},{3,11},{4,12},{5,13},{6,14},{7,15},{8,0},{9,1},... | collective-permute-start | bytes 786440 | tf_op jit(solution)/shard_map/ppermute | solution.py:18
  52.3 6.7 %collective-permute-start.4 = (bf16[2,2,2,2,4,2048]{5,4,3,2,1,0:T(4,128)(2,1)}, bf16[2,2,2,2,4,2048]{5,4,3,2,1,0:T(4,128)(2,1)}, u32[]{:S(2)}, u32[]{:S(2)}) collective-permute-start(bf16[2,2,2,2,4,2048]{5,4,3,2,1,0:T(4,128)(2,1)} %pad_maximum_fusion.1), channel_id=1, source_target_pairs={{0,1},{1,0},{2,3},{3,2},{4,5},{5,4},{6,7},{7,6},{8,9},{9,8},{10,11... | collective-permute-start | bytes 786440 | tf_op jit(solution)/shard_map/ppermute | solution.py:18
  63.3 3.4 %copy-start.1 = (bf16[4,32,4096]{2,1,0:T(8,128)(2,1)}, bf16[4,32,4096]{2,1,0:T(8,128)(2,1)S(1)}, u32[]{:S(2)}) copy-start(bf16[4,32,4096]{2,1,0:T(8,128)(2,1)S(1)} %constant_dynamic-update-slice_fusion) | copy-start | bytes 3145732
  66.7 1.7 copy-start.16
  66.7 1.7 copy-start.20
  83.4 25.5 %copy-start.12 = (pred[4,512]{1,0:T(4,128)(4,1)S(1)}, pred[4,512]{1,0:T(4,128)(4,1)}, u32[]{:S(2)}) copy-start(pred[4,512]{1,0:T(4,128)(4,1)} %iota_compare_fusion.7) | copy-start | bytes 6148
  83.5 25.6 %copy-start.17 = (pred[32]{0:T(512)(128)(4,1)S(1)}, pred[32]{0:T(512)(128)(4,1)}, u32[]{:S(2)}) copy-start(pred[32]{0:T(512)(128)(4,1)} %broadcast_in_dim.247) | copy-start | bytes 100
  83.5 9.2 %collective-permute-start.11 = (f32[4,8,32,4]{1,3,0,2:T(4,128)S(1)}, f32[4,8,32,4]{1,3,0,2:T(4,128)S(1)}, u32[]{:S(2)}, u32[]{:S(2)}) collective-permute-start(f32[4,8,32,4]{1,3,0,2:T(4,128)S(1)} %convolution_bitcast_fusion.4), channel_id=1, source_target_pairs={{0,1},{1,0},{2,3},{3,2},{4,5},{5,4},{6,7},{7,6},{8,9},{9,8},{10,11... | collective-permute-start | bytes 49160 | tf_op jit(solution)/shard_map/ppermute | solution.py:18
  86.1 17.9 %collective-permute-start.10 = (f32[4,8,32,64]{3,1,0,2:T(8,128)S(1)}, f32[4,8,32,64]{3,1,0,2:T(8,128)S(1)}, u32[]{:S(2)}, u32[]{:S(2)}) collective-permute-start(f32[4,8,32,64]{3,1,0,2:T(8,128)S(1)} %convolution_bitcast_fusion.2), channel_id=1, source_target_pairs={{0,1},{1,0},{2,3},{3,2},{4,5},{5,4},{6,7},{7,6},{8,9},{9,8},{10,11... | collective-permute-start | bytes 786440 | tf_op jit(solution)/shard_map/ppermute | solution.py:18
  88.4 20.5 %collective-permute-start.12 = (f32[4,8,4,512]{3,1,0,2:T(8,128)S(1)}, f32[4,8,4,512]{3,1,0,2:T(8,128)S(1)}, u32[]{:S(2)}, u32[]{:S(2)}) collective-permute-start(f32[4,8,4,512]{3,1,0,2:T(8,128)S(1)} %convolution_bitcast_fusion.3), channel_id=1, source_target_pairs={{0,1},{1,0},{2,3},{3,2},{4,5},{5,4},{6,7},{7,6},{8,9},{9,8},{10,11... | collective-permute-start | bytes 786440 | tf_op jit(solution)/shard_map/ppermute | solution.py:18
  92.7 0.7 copy-start.7
  103.9 5.0 %copy-start.5 = (f32[4,8,32,64]{3,1,0,2:T(8,128)}, f32[4,8,32,64]{3,1,0,2:T(8,128)S(1)}, u32[]{:S(2)}) copy-start(f32[4,8,32,64]{3,1,0,2:T(8,128)S(1)} %collective-permute-done.10) | copy-start | bytes 786436
  104.4 21.4 %copy-start.18 = (pred[32]{0:T(512)(128)(4,1)S(1)}, pred[32]{0:T(512)(128)(4,1)}, u32[]{:S(2)}) copy-start(pred[32]{0:T(512)(128)(4,1)} %broadcast_in_dim.247) | copy-start | bytes 100
  111.9 19.2 %copy-start.13 = (pred[4,512]{1,0:T(4,128)(4,1)S(1)}, pred[4,512]{1,0:T(4,128)(4,1)}, u32[]{:S(2)}) copy-start(pred[4,512]{1,0:T(4,128)(4,1)} %iota_compare_fusion.7) | copy-start | bytes 6148
  133.5 1.8 copy-start.8
  133.5 1.8 copy-start.11
  133.6 1.8 copy-start.14
  135.3 1.0 copy-start.3
  135.3 1.2 copy-start.4
  138.1 19.0 %all-to-all-start = ((f32[4,8,32,130]{3,0,2,1:T(4,128)}), f32[4,8,32,130]{3,0,2,1:T(4,128)S(1)}, u32[]{:S(2)}, u32[]{:S(2)}) async-start(f32[4,8,32,130]{3,0,2,1:T(4,128)} %copy.500), calls=%async_computation | async-start | bytes 2097152 | tf_op jit(solution)/shard_map/all_to_all | solution.py:243
  161.1 3.8 %copy-start.19 = (f32[256]{0:T(256)S(1)}, f32[256]{0:T(256)}, u32[]{:S(2)}) copy-start(f32[256]{0:T(256)} %param.20) | copy-start | bytes 3076
  161.8 3.2 %copy-start.2 = (bf16[4,32,4096]{2,1,0:T(8,128)(2,1)S(1)}, bf16[4,32,4096]{2,1,0:T(8,128)(2,1)}, u32[]{:S(2)}) copy-start(bf16[4,32,4096]{2,1,0:T(8,128)(2,1)} %copy-done.1) | copy-start | bytes 3145732
  177.9 13.7 %collective-permute-start.13 = (f32[2,2,2,2,4,2048]{5,4,3,2,0,1:T(4,128)}, f32[2,2,2,2,4,2048]{5,4,3,2,0,1:T(4,128)}, u32[]{:S(2)}, u32[]{:S(2)}) collective-permute-start(f32[2,2,2,2,4,2048]{5,4,3,2,0,1:T(4,128)} %bitcast.296), channel_id=1, source_target_pairs={{0,1},{1,0},{2,3},{3,2},{4,5},{5,4},{6,7},{7,6},{8,9},{9,8},{10,11... | collective-permute-start | bytes 1572872 | tf_op jit(solution)/shard_map/ppermute | solution.py:18
  180.8 10.7 %copy-start.6 = (f32[2,2,2,2,1,4,2048]{6,4,3,2,1,0,5:T(1,128)S(1)}, f32[2,2,2,2,1,4,2048]{6,4,3,2,1,0,5:T(1,128)}, u32[]{:S(2)}) copy-start(f32[2,2,2,2,1,4,2048]{6,4,3,2,1,0,5:T(1,128)} %get-tuple-element.18) | copy-start | bytes 1572868
  181.3 13.8 %collective-permute-start.18 = (f32[2,2,2,2,4,2048]{5,4,2,1,0,3:T(4,128)S(1)}, f32[2,2,2,2,4,2048]{5,4,2,1,0,3:T(4,128)S(1)}, u32[]{:S(2)}, u32[]{:S(2)}) collective-permute-start(f32[2,2,2,2,4,2048]{5,4,2,1,0,3:T(4,128)S(1)} %bitcast.306), channel_id=1, source_target_pairs={{0,8},{1,9},{2,10},{3,11},{4,12},{5,13},{6,14},{7,15},{8,0},{9,1},... | collective-permute-start | bytes 1572872 | tf_op jit(solution)/shard_map/ppermute | solution.py:18
  193.0 7.3 %collective-permute-start.14 = (f32[2,2,2,4,2048]{4,3,2,1,0:T(4,128)S(1)}, f32[2,2,2,4,2048]{4,3,2,1,0:T(4,128)S(1)}, u32[]{:S(2)}, u32[]{:S(2)}) collective-permute-start(f32[2,2,2,4,2048]{4,3,2,1,0:T(4,128)S(1)} %dynamic-slice_bitcast_fusion.1), channel_id=1, source_target_pairs={{0,8},{1,9},{2,10},{3,11},{4,12},{5,13},{6,14},{7,15},{8,0},{9,1},... | collective-permute-start | bytes 786440 | tf_op jit(solution)/shard_map/ppermute | solution.py:18
  195.5 28.3 %copy-start.9 = (bf16[4,1,1,4096]{3,0,2,1:T(4,128)(2,1)S(1)}, bf16[4,1,1,4096]{3,0,2,1:T(4,128)(2,1)}, u32[]{:S(2)}) copy-start(bf16[4,1,1,4096]{3,0,2,1:T(4,128)(2,1)} %param.14) | copy-start | bytes 98308
  195.5 28.3 %copy-start.15 = (f32[4096]{0:T(1024)S(1)}, f32[4096]{0:T(1024)}, u32[]{:S(2)}) copy-start(f32[4096]{0:T(1024)} %param.22) | copy-start | bytes 49156
  195.6 6.5 %collective-permute-start.19 = (f32[2,2,2,4,2048]{4,3,2,1,0:T(4,128)S(1)}, f32[2,2,2,4,2048]{4,3,2,1,0:T(4,128)S(1)}, u32[]{:S(2)}, u32[]{:S(2)}) collective-permute-start(f32[2,2,2,4,2048]{4,3,2,1,0:T(4,128)S(1)} %dynamic-slice_bitcast_fusion), channel_id=1, source_target_pairs={{0,1},{1,0},{2,3},{3,2},{4,5},{5,4},{6,7},{7,6},{8,9},{9,8},{10,11... | collective-permute-start | bytes 786440 | tf_op jit(solution)/shard_map/ppermute | solution.py:18
  200.5 7.4 %collective-permute-start.15 = (f32[2,2,4,2048]{3,2,1,0:T(4,128)S(1)}, f32[2,2,4,2048]{3,2,1,0:T(4,128)S(1)}, u32[]{:S(2)}, u32[]{:S(2)}) collective-permute-start(f32[2,2,4,2048]{3,2,1,0:T(4,128)S(1)} %dynamic-slice_bitcast_fusion.3), channel_id=1, source_target_pairs={{0,2},{1,3},{2,0},{3,1},{4,6},{5,7},{6,4},{7,5},{8,10},{9,11},{10,... | collective-permute-start | bytes 393224 | tf_op jit(solution)/shard_map/ppermute | solution.py:18
  202.2 7.8 %collective-permute-start.20 = (f32[2,2,4,2048]{3,2,1,0:T(4,128)S(1)}, f32[2,2,4,2048]{3,2,1,0:T(4,128)S(1)}, u32[]{:S(2)}, u32[]{:S(2)}) collective-permute-start(f32[2,2,4,2048]{3,2,1,0:T(4,128)S(1)} %dynamic-slice_bitcast_fusion.2), channel_id=1, source_target_pairs={{0,16},{1,17},{2,18},{3,19},{4,20},{5,21},{6,22},{7,23},{8,24},{9,... | collective-permute-start | bytes 393224 | tf_op jit(solution)/shard_map/ppermute | solution.py:18
  207.9 5.9 %collective-permute-start.16 = (f32[2,4,2048]{2,1,0:T(4,128)S(1)}, f32[2,4,2048]{2,1,0:T(4,128)S(1)}, u32[]{:S(2)}, u32[]{:S(2)}) collective-permute-start(f32[2,4,2048]{2,1,0:T(4,128)S(1)} %dynamic-slice_bitcast_fusion.5), channel_id=1, source_target_pairs={{0,16},{1,17},{2,18},{3,19},{4,20},{5,21},{6,22},{7,23},{8,24},{9,... | collective-permute-start | bytes 196616 | tf_op jit(solution)/shard_map/ppermute | solution.py:18
  210.0 5.8 %collective-permute-start.21 = (f32[2,4,2048]{2,1,0:T(4,128)S(1)}, f32[2,4,2048]{2,1,0:T(4,128)S(1)}, u32[]{:S(2)}, u32[]{:S(2)}) collective-permute-start(f32[2,4,2048]{2,1,0:T(4,128)S(1)} %dynamic-slice_bitcast_fusion.4), channel_id=1, source_target_pairs={{0,2},{1,3},{2,0},{3,1},{4,6},{5,7},{6,4},{7,5},{8,10},{9,11},{10,... | collective-permute-start | bytes 196616 | tf_op jit(solution)/shard_map/ppermute | solution.py:18
  213.8 7.9 %collective-permute-start.17 = (f32[4,2048]{1,0:T(4,128)S(1)}, f32[4,2048]{1,0:T(4,128)S(1)}, u32[]{:S(2)}, u32[]{:S(2)}) collective-permute-start(f32[4,2048]{1,0:T(4,128)S(1)} %dynamic-slice_bitcast_fusion.7), channel_id=1, source_target_pairs={{0,4},{1,5},{2,6},{3,7},{4,0},{5,1},{6,2},{7,3},{8,12},{9,13},{10,... | collective-permute-start | bytes 98312 | tf_op jit(solution)/shard_map/ppermute | solution.py:18
  215.9 7.9 %collective-permute-start.22 = (f32[4,2048]{1,0:T(4,128)S(1)}, f32[4,2048]{1,0:T(4,128)S(1)}, u32[]{:S(2)}, u32[]{:S(2)}) collective-permute-start(f32[4,2048]{1,0:T(4,128)S(1)} %dynamic-slice_bitcast_fusion.6), channel_id=1, source_target_pairs={{0,4},{1,5},{2,6},{3,7},{4,0},{5,1},{6,2},{7,3},{8,12},{9,13},{10,... | collective-permute-start | bytes 98312 | tf_op jit(solution)/shard_map/ppermute | solution.py:18

commit v4 on v3

--- a/solution.py
+++ b/solution.py
@@ -10,6 +10,7 @@
 BEAMS = 8
 
 NEG_FILL = -1e30
+LINK_TYPE = jnp.bfloat16
 SCATTER_ORDERS = ((0, 3, 1, 4, 2), (3, 0, 4, 1, 2))
 GATHER_ORDERS = ((2, 4, 1, 3, 0), (2, 1, 4, 0, 3))
 
@@ -28,8 +29,8 @@
         a = remaining.index(k)
         bit = (me >> k) & 1
         keep = lax.dynamic_index_in_dim(x, bit, a, keepdims=False)
-        send = lax.dynamic_index_in_dim(x, 1 - bit, a, keepdims=False)
-        x = keep + partner(send, axis, k)
+        send = lax.dynamic_index_in_dim(x, 1 - bit, a, keepdims=False).astype(LINK_TYPE)
+        x = keep + partner(send, axis, k).astype(keep.dtype)
         remaining.pop(a)
     return x
 

time: 226 us -> 220 us (0.973)
  waiting for transfers between devices: 75.9 us -> 67.4 us
  local copies, waits for them, and re-layouts: 47.5 us -> 50.6 us
    ppermute x23, waiting for transfers between devices: 61.5 us -> 52.9 us  [partner(): lax.ppermute(value, axis, [(i, i ^ 1 << bit) for i in range(lax.axis_size...]
    unnamed x52 -> x56, local copies, waits for them, and re-layouts: 10.4 us -> 10.9 us
  transfers between devices with their start and end apart: 24 -> 24, of which waited for: 20 -> 19; matrix products, arithmetic and copies ran while one was open for 11% -> 13% of each run, Pallas kernels for 0% -> 0%
where the time goes in v4:
time: 220 us; the launch traced here: 218 us
  waiting for transfers between devices  67.4 us (31%)
  local copies, waits for them, and re-layouts  50.6 us (23%)
  starting transfers between devices  42 us (19%)
  other arithmetic  25.8 us (12%)
  matrix products  18.8 us (9%)
  blocking collectives  12.9 us (6%)
    ppermute x23, waiting for transfers between devices, partner(): lax.ppermute(value, axis, [(i, i ^ 1 << bit) for i in range(lax.axis_size...  52.9 us
    ppermute x23, starting transfers between devices, partner(): lax.ppermute(value, axis, [(i, i ^ 1 << bit) for i in range(lax.axis_size...  37.5 us
    all_to_all x1, waiting for transfers between devices, on_device(): received = lax.all_to_all(packed, 'batch', 1, 1, tiled=True)  14.5 us
    all_gather x1, blocking collectives, on_device(): query_all = lax.all_gather(queries[:, None], 'batch', axis=1, tiled=True)  12.9 us
    unnamed x56, local copies, waits for them, and re-layouts  10.9 us
    broadcast_in_dim x6, local copies, waits for them, and re-layouts, spread(): placed = jnp.where(slot_hit, values[..., None], fill)  6.56 us
    dot_general x1, matrix products, on_device(): jnp.einsum('srf,fd->rsd', hidden, down_weight, preferred_element_type=jnp...  4.9 us
    all_to_all x1, starting transfers between devices, on_device(): received = lax.all_to_all(packed, 'batch', 1, 1, tiled=True)  4.51 us
  transfers between devices with their start and end apart: 24, of which 19 were waited for; matrix products, arithmetic and copies ran while one was open for 13% of the time, Pallas kernels for 0%

profile of v4, /device:TPU:2, one launch (start us, length us, event | category | flops | bytes accessed | tf_op | source)
XLA Modules:
  0.0 218.2 jit_solution(9596680367402503526)
XLA Ops:
  3.8 7.3 %collective-permute-start.5 = (bf16[4,2048]{1,0:T(4,128)(2,1)S(1)}, bf16[4,2048]{1,0:T(4,128)(2,1)S(1)}, u32[]{:S(2)}, u32[]{:S(2)}) collective-permute-start(bf16[4,2048]{1,0:T(4,128)(2,1)S(1)} %slice.98), channel_id=1, source_target_pairs={{0,4},{1,5},{2,6},{3,7},{4,0},{5,1},{6,2},{7,3},{8,12},{9,13},{10,... | collective-permute-start | bytes 49160 | tf_op jit(solution)/shard_map/ppermute | solution.py:19
  15.1 2.0 gather_fusion
  19.7 4.7 %copy.469 = bf16[4096,3,128]{0,2,1:T(8,128)(2,1)} copy(bf16[4096,3,128]{2,0,1:T(8,128)(2,1)} %param.17) | data formatting | bytes 6291456 | tf_op args[3]
  25.6 2.1 collective-permute-start.6
  27.6 5.7 %collective-permute-done = bf16[4,2048]{1,0:T(4,128)(2,1)S(1)} collective-permute-done((bf16[4,2048]{1,0:T(4,128)(2,1)S(1)}, bf16[4,2048]{1,0:T(4,128)(2,1)S(1)}, u32[]{:S(2)}, u32[]{:S(2)}) %collective-permute-start) | collective-permute-done | bytes 16416 | tf_op jit(solution)/shard_map/ppermute | solution.py:19
  33.4 3.3 %collective-permute-start.1 = (bf16[2,4,2048]{2,1,0:T(4,128)(2,1)S(1)}, bf16[2,4,2048]{2,1,0:T(4,128)(2,1)S(1)}, u32[]{:S(2)}, u32[]{:S(2)}) collective-permute-start(bf16[2,4,2048]{2,1,0:T(4,128)(2,1)S(1)} %pad_maximum_fusion.9), channel_id=1, source_target_pairs={{0,16},{1,17},{2,18},{3,19},{4,20},{5,21},{6,22},{7,23},{8,24},{9,... | collective-permute-start | bytes 98312 | tf_op jit(solution)/shard_map/ppermute | solution.py:19
  37.2 1.7 collective-permute-done.1
  40.4 2.3 %collective-permute-done.7 = bf16[2,2,4,2048]{3,2,1,0:T(4,128)(2,1)S(1)} collective-permute-done((bf16[2,2,4,2048]{3,2,1,0:T(4,128)(2,1)S(1)}, bf16[2,2,4,2048]{3,2,1,0:T(4,128)(2,1)S(1)}, u32[]{:S(2)}, u32[]{:S(2)}) %collective-permute-start.7) | collective-permute-done | bytes 65568 | tf_op jit(solution)/shard_map/ppermute | solution.py:19
  44.8 1.6 collective-permute-start.3
  46.4 1.4 collective-permute-done.8
  49.0 2.3 %collective-permute-done.3 = bf16[2,2,2,4,2048]{4,3,2,1,0:T(4,128)(2,1)S(1)} collective-permute-done((bf16[2,2,2,4,2048]{4,3,2,1,0:T(4,128)(2,1)S(1)}, bf16[2,2,2,4,2048]{4,3,2,1,0:T(4,128)(2,1)S(1)}, u32[]{:S(2)}, u32[]{:S(2)}) %collective-permute-start.3) | collective-permute-done | bytes 131104 | tf_op jit(solution)/shard_map/ppermute | solution.py:19
  56.1 2.9 %collective-permute-done.4 = bf16[2,2,2,2,4,2048]{5,4,3,2,1,0:T(4,128)(2,1)} collective-permute-done((bf16[2,2,2,2,4,2048]{5,4,3,2,1,0:T(4,128)(2,1)}, bf16[2,2,2,2,4,2048]{5,4,3,2,1,0:T(4,128)(2,1)}, u32[]{:S(2)}, u32[]{:S(2)}) %collective-permute-start.4) | collective-permute-done | bytes 262176 | tf_op jit(solution)/shard_map/ppermute | solution.py:19
  63.4 3.3 %fusion.121 = f32[4,32,384]{2,1,0:T(8,128)S(1)} fusion(bf16[4,32,4096]{2,1,0:T(8,128)(2,1)S(1)} %constant_dynamic-update-slice_fusion, bf16[4096,384,1]{0,1,2:T(8,128)(2,1)} %bitcast.297), kind=kOutput, calls=%fused_computation.258 | convolution fusion | flops 402653184 | bytes 4390912 | tf_op jit(solution)/shard_map/dot_general | solution.py:130
  69.1 12.9 %all_gather.3 = bf16[4,8,32,128]{3,2,0,1:T(8,128)(2,1)S(1)} all-gather(bf16[4,1,32,128]{3,2,0,1:T(8,128)(2,1)S(1)} %copy.475), channel_id=1, replica_groups=mesh['batch'=8,'tensor'=32] {'batch'}, dimensions={1}, use_global_device_ids=true | all-gather | bytes 294912 | tf_op jit(solution)/shard_map/all_gather | solution.py:147
  84.7 1.4 convolution_bitcast_fusion.2
  88.5 1.4 collective-permute-start.12
  89.9 2.9 %collective-permute-done.11 = f32[4,8,32,4]{1,3,0,2:T(4,128)S(1)} collective-permute-done((f32[4,8,32,4]{1,3,0,2:T(4,128)S(1)}, f32[4,8,32,4]{1,3,0,2:T(4,128)S(1)}, u32[]{:S(2)}, u32[]{:S(2)}) %collective-permute-start.11) | collective-permute-done | bytes 16416 | tf_op jit(solution)/shard_map/ppermute | solution.py:19
  93.7 10.2 %collective-permute-done.10 = f32[4,8,32,64]{3,1,0,2:T(8,128)S(1)} collective-permute-done((f32[4,8,32,64]{3,1,0,2:T(8,128)S(1)}, f32[4,8,32,64]{3,1,0,2:T(8,128)S(1)}, u32[]{:S(2)}, u32[]{:S(2)}) %collective-permute-start.10) | collective-permute-done | bytes 262176 | tf_op jit(solution)/shard_map/ppermute | solution.py:19
  104.4 4.5 %collective-permute-done.12 = f32[4,8,4,512]{3,1,0,2:T(8,128)S(1)} collective-permute-done((f32[4,8,4,512]{3,1,0,2:T(8,128)S(1)}, f32[4,8,4,512]{3,1,0,2:T(8,128)S(1)}, u32[]{:S(2)}, u32[]{:S(2)}) %collective-permute-start.12) | collective-permute-done | bytes 262176 | tf_op jit(solution)/shard_map/ppermute | solution.py:19
  113.3 1.6 fusion.18
  115.5 1.5 copy.499
  117.0 1.5 fusion.28
  118.5 1.4 copy.500
  119.8 1.4 broadcast_in_dim.262
  121.3 1.5 broadcast_in_dim.263
  122.8 1.4 broadcast_in_dim.251
  124.2 1.5 broadcast_in_dim.260
  127.2 2.0 copy.502
  129.1 2.0 copy.503
  133.6 1.7 convolution_bitcast_fusion.1
  138.1 4.5 %all-to-all-start = ((f32[4,8,32,130]{3,0,2,1:T(4,128)}), f32[4,8,32,130]{3,0,2,1:T(4,128)S(1)}, u32[]{:S(2)}, u32[]{:S(2)}) async-start(f32[4,8,32,130]{3,0,2,1:T(4,128)} %copy.504), calls=%async_computation | async-start | bytes 2097152 | tf_op jit(solution)/shard_map/all_to_all | solution.py:244
  142.6 14.5 %all-to-all-done = f32[4,8,32,130]{3,0,2,1:T(4,128)S(1)} async-done(((f32[4,8,32,130]{3,0,2,1:T(4,128)}), f32[4,8,32,130]{3,0,2,1:T(4,128)S(1)}, u32[]{:S(2)}, u32[]{:S(2)}) %all-to-all-start) | async-done | bytes 532512 | tf_op jit(solution)/shard_map/all_to_all | solution.py:244
  161.9 3.0 %fusion.10 = f32[4,32,4096]{2,1,0:T(8,128)} fusion(bf16[128,4096]{1,0:T(8,128)(2,1)} %param.18, bf16[4,32,128]{2,0,1:T(4,128)(2,1)S(1)} %divide_convert_fusion), kind=kOutput, calls=%fused_computation.17 | convolution fusion | flops 134217728 | bytes 3178496 | tf_op jit(solution)/shard_map/src,cd->rsd/dot_general | solution.py:254
  164.9 4.9 %fusion = f32[32,4,4096]{2,0,1:T(8,128)} fusion(f32[4,32,4096]{2,1,0:T(8,128)} %fusion.10, bf16[256,4096]{1,0:T(8,128)(2,1)S(1)} %copy-done, bf16[4,32,4096]{2,1,0:T(8,128)(2,1)S(1)} %copy-done.2, bf16[4096,256]{1,0:T(8,128)(2,1)} %param.19, f32[256]{0:T(256)S(1)} %copy-done.20), kind=kOutput, calls=%fused_computation.2 | convolution fusion | flops 537722880 | bytes 9438208 | tf_op jit(solution)/shard_map/srf,fd->rsd/dot_general | solution.py:256
  169.8 2.7 %fusion.115 = (f32[32,4,2048]{2,0,1:T(8,128)}, f32[32,4,2048]{2,0,1:T(8,128)S(1)}) fusion(f32[32,4,4096]{2,0,1:T(8,128)} %fusion), kind=kLoop, calls=%fused_computation.252 | loop fusion | bytes 4194304 | tf_op jit(solution)/shard_map/slice | solution.py:59
  172.5 2.8 %reshape.509 = f32[2,2,2,2,2,4,2048]{6,4,3,2,1,0,5:T(2,128)} reshape(f32[32,4,2048]{2,0,1:T(8,128)} %get-tuple-element.16) | data formatting | bytes 2097152 | tf_op jit(solution)/shard_map/reshape | solution.py:26
  175.4 1.9 constant_dynamic-slice_fusion.2
  180.2 1.6 reshape.510
  188.3 4.2 %collective-permute-done.18 = bf16[2,2,2,2,4,2048]{5,4,1,2,0,3:T(4,128)(2,1)S(1)} collective-permute-done((bf16[2,2,2,2,4,2048]{5,4,1,2,0,3:T(4,128)(2,1)S(1)}, bf16[2,2,2,2,4,2048]{5,4,1,2,0,3:T(4,128)(2,1)S(1)}, u32[]{:S(2)}, u32[]{:S(2)}) %collective-permute-start.18) | collective-permute-done | bytes 262176 | tf_op jit(solution)/shard_map/ppermute | solution.py:19
  194.1 1.7 collective-permute-start.15
  195.8 2.6 %collective-permute-done.19 = bf16[2,2,2,4,2048]{4,3,1,2,0:T(4,128)(2,1)S(1)} collective-permute-done((bf16[2,2,2,4,2048]{4,3,1,2,0:T(4,128)(2,1)S(1)}, bf16[2,2,2,4,2048]{4,3,1,2,0:T(4,128)(2,1)S(1)}, u32[]{:S(2)}, u32[]{:S(2)}) %collective-permute-start.19) | collective-permute-done | bytes 131104 | tf_op jit(solution)/shard_map/ppermute | solution.py:19
  200.1 2.3 %collective-permute-start.16 = (bf16[2,4,2048]{2,1,0:T(4,128)(2,1)S(1)}, bf16[2,4,2048]{2,1,0:T(4,128)(2,1)S(1)}, u32[]{:S(2)}, u32[]{:S(2)}) collective-permute-start(bf16[2,4,2048]{2,1,0:T(4,128)(2,1)S(1)} %fusion.88), channel_id=1, source_target_pairs={{0,16},{1,17},{2,18},{3,19},{4,20},{5,21},{6,22},{7,23},{8,24},{9,... | collective-permute-start | bytes 98312 | tf_op jit(solution)/shard_map/ppermute | solution.py:19
  202.4 1.9 collective-permute-done.20
  205.7 1.5 collective-permute-start.17
  207.2 2.4 %collective-permute-done.21 = bf16[2,4,2048]{2,1,0:T(4,128)(2,1)S(1)} collective-permute-done((bf16[2,4,2048]{2,1,0:T(4,128)(2,1)S(1)}, bf16[2,4,2048]{2,1,0:T(4,128)(2,1)S(1)}, u32[]{:S(2)}, u32[]{:S(2)}) %collective-permute-start.21) | collective-permute-done | bytes 32800 | tf_op jit(solution)/shard_map/ppermute | solution.py:19
  209.7 2.2 %collective-permute-start.22 = (bf16[4,2048]{1,0:T(4,128)(2,1)S(1)}, bf16[4,2048]{1,0:T(4,128)(2,1)S(1)}, u32[]{:S(2)}, u32[]{:S(2)}) collective-permute-start(bf16[4,2048]{1,0:T(4,128)(2,1)S(1)} %fusion.94), channel_id=1, source_target_pairs={{0,4},{1,5},{2,6},{3,7},{4,0},{5,1},{6,2},{7,3},{8,12},{9,13},{10,... | collective-permute-start | bytes 49160 | tf_op jit(solution)/shard_map/ppermute | solution.py:19
  211.9 1.6 collective-permute-done.17
  213.5 3.9 %collective-permute-done.22 = bf16[4,2048]{1,0:T(4,128)(2,1)S(1)} collective-permute-done((bf16[4,2048]{1,0:T(4,128)(2,1)S(1)}, bf16[4,2048]{1,0:T(4,128)(2,1)S(1)}, u32[]{:S(2)}, u32[]{:S(2)}) %collective-permute-start.22) | collective-permute-done | bytes 16416 | tf_op jit(solution)/shard_map/ppermute | solution.py:19
  (204 shorter events, 65.9 us)
Async XLA Ops:
  0.0 164.9 %copy-start = (bf16[256,4096]{1,0:T(8,128)(2,1)S(1)}, bf16[256,4096]{1,0:T(8,128)(2,1)}, u32[]{:S(2)}) copy-start(bf16[256,4096]{1,0:T(8,128)(2,1)} %param.21) | copy-start | bytes 6291460
  3.8 21.6 %collective-permute-start.5 = (bf16[4,2048]{1,0:T(4,128)(2,1)S(1)}, bf16[4,2048]{1,0:T(4,128)(2,1)S(1)}, u32[]{:S(2)}, u32[]{:S(2)}) collective-permute-start(bf16[4,2048]{1,0:T(4,128)(2,1)S(1)} %slice.98), channel_id=1, source_target_pairs={{0,4},{1,5},{2,6},{3,7},{4,0},{5,1},{6,2},{7,3},{8,12},{9,13},{10,... | collective-permute-start | bytes 49160 | tf_op jit(solution)/shard_map/ppermute | solution.py:19
  24.7 79.2 %copy-start.11 = (pred[4,8,32]{1,0,2:T(4,128)(4,1)}, pred[4,8,32]{1,0,2:T(4,128)(4,1)S(1)}, u32[]{:S(2)}) copy-start(pred[4,8,32]{1,0,2:T(4,128)(4,1)S(1)} %copy.466) | copy-start | bytes 3076
  25.4 7.9 %collective-permute-start = (bf16[4,2048]{1,0:T(4,128)(2,1)S(1)}, bf16[4,2048]{1,0:T(4,128)(2,1)S(1)}, u32[]{:S(2)}, u32[]{:S(2)}) collective-permute-start(bf16[4,2048]{1,0:T(4,128)(2,1)S(1)} %get-tuple-element.55), channel_id=1, source_target_pairs={{0,4},{1,5},{2,6},{3,7},{4,0},{5,1},{6,2},{7,3},{8,12},{9,13},{10,... | collective-permute-start | bytes 49160 | tf_op jit(solution)/shard_map/ppermute | solution.py:19
  25.6 11.1 %collective-permute-start.6 = (bf16[2,4,2048]{2,1,0:T(4,128)(2,1)S(1)}, bf16[2,4,2048]{2,1,0:T(4,128)(2,1)S(1)}, u32[]{:S(2)}, u32[]{:S(2)}) collective-permute-start(bf16[2,4,2048]{2,1,0:T(4,128)(2,1)S(1)} %pad_maximum_fusion.10), channel_id=1, source_target_pairs={{0,2},{1,3},{2,0},{3,1},{4,6},{5,7},{6,4},{7,5},{8,10},{9,11},{10,... | collective-permute-start | bytes 98312 | tf_op jit(solution)/shard_map/ppermute | solution.py:19
  33.4 5.5 %collective-permute-start.1 = (bf16[2,4,2048]{2,1,0:T(4,128)(2,1)S(1)}, bf16[2,4,2048]{2,1,0:T(4,128)(2,1)S(1)}, u32[]{:S(2)}, u32[]{:S(2)}) collective-permute-start(bf16[2,4,2048]{2,1,0:T(4,128)(2,1)S(1)} %pad_maximum_fusion.9), channel_id=1, source_target_pairs={{0,16},{1,17},{2,18},{3,19},{4,20},{5,21},{6,22},{7,23},{8,24},{9,... | collective-permute-start | bytes 98312 | tf_op jit(solution)/shard_map/ppermute | solution.py:19
  36.8 5.9 %collective-permute-start.7 = (bf16[2,2,4,2048]{3,2,1,0:T(4,128)(2,1)S(1)}, bf16[2,2,4,2048]{3,2,1,0:T(4,128)(2,1)S(1)}, u32[]{:S(2)}, u32[]{:S(2)}) collective-permute-start(bf16[2,2,4,2048]{3,2,1,0:T(4,128)(2,1)S(1)} %pad_maximum_fusion.6), channel_id=1, source_target_pairs={{0,16},{1,17},{2,18},{3,19},{4,20},{5,21},{6,22},{7,23},{8,24},{9,... | collective-permute-start | bytes 196616 | tf_op jit(solution)/shard_map/ppermute | solution.py:19
  39.0 5.7 %collective-permute-start.2 = (bf16[2,2,4,2048]{3,2,1,0:T(4,128)(2,1)S(1)}, bf16[2,2,4,2048]{3,2,1,0:T(4,128)(2,1)S(1)}, u32[]{:S(2)}, u32[]{:S(2)}) collective-permute-start(bf16[2,2,4,2048]{3,2,1,0:T(4,128)(2,1)S(1)} %pad_maximum_fusion.5), channel_id=1, source_target_pairs={{0,2},{1,3},{2,0},{3,1},{4,6},{5,7},{6,4},{7,5},{8,10},{9,11},{10,... | collective-permute-start | bytes 196616 | tf_op jit(solution)/shard_map/ppermute | solution.py:19
  42.8 5.1 %collective-permute-start.8 = (bf16[2,2,2,4,2048]{4,3,2,1,0:T(4,128)(2,1)S(1)}, bf16[2,2,2,4,2048]{4,3,2,1,0:T(4,128)(2,1)S(1)}, u32[]{:S(2)}, u32[]{:S(2)}) collective-permute-start(bf16[2,2,2,4,2048]{4,3,2,1,0:T(4,128)(2,1)S(1)} %pad_maximum_fusion.4), channel_id=1, source_target_pairs={{0,1},{1,0},{2,3},{3,2},{4,5},{5,4},{6,7},{7,6},{8,9},{9,8},{10,11... | collective-permute-start | bytes 393224 | tf_op jit(solution)/shard_map/ppermute | solution.py:19
  44.8 6.5 %collective-permute-start.3 = (bf16[2,2,2,4,2048]{4,3,2,1,0:T(4,128)(2,1)S(1)}, bf16[2,2,2,4,2048]{4,3,2,1,0:T(4,128)(2,1)S(1)}, u32[]{:S(2)}, u32[]{:S(2)}) collective-permute-start(bf16[2,2,2,4,2048]{4,3,2,1,0:T(4,128)(2,1)S(1)} %pad_maximum_fusion.3), channel_id=1, source_target_pairs={{0,8},{1,9},{2,10},{3,11},{4,12},{5,13},{6,14},{7,15},{8,0},{9,1},... | collective-permute-start | bytes 393224 | tf_op jit(solution)/shard_map/ppermute | solution.py:19
  48.2 6.5 %collective-permute-start.9 = (bf16[2,2,2,2,4,2048]{5,4,3,2,1,0:T(4,128)(2,1)S(1)}, bf16[2,2,2,2,4,2048]{5,4,3,2,1,0:T(4,128)(2,1)S(1)}, u32[]{:S(2)}, u32[]{:S(2)}) collective-permute-start(bf16[2,2,2,2,4,2048]{5,4,3,2,1,0:T(4,128)(2,1)S(1)} %pad_maximum_fusion.2), channel_id=1, source_target_pairs={{0,8},{1,9},{2,10},{3,11},{4,12},{5,13},{6,14},{7,15},{8,0},{9,1},... | collective-permute-start | bytes 786440 | tf_op jit(solution)/shard_map/ppermute | solution.py:19
  52.4 6.7 %collective-permute-start.4 = (bf16[2,2,2,2,4,2048]{5,4,3,2,1,0:T(4,128)(2,1)}, bf16[2,2,2,2,4,2048]{5,4,3,2,1,0:T(4,128)(2,1)}, u32[]{:S(2)}, u32[]{:S(2)}) collective-permute-start(bf16[2,2,2,2,4,2048]{5,4,3,2,1,0:T(4,128)(2,1)} %pad_maximum_fusion.1), channel_id=1, source_target_pairs={{0,1},{1,0},{2,3},{3,2},{4,5},{5,4},{6,7},{7,6},{8,9},{9,8},{10,11... | collective-permute-start | bytes 786440 | tf_op jit(solution)/shard_map/ppermute | solution.py:19
  63.4 3.4 %copy-start.1 = (bf16[4,32,4096]{2,1,0:T(8,128)(2,1)}, bf16[4,32,4096]{2,1,0:T(8,128)(2,1)S(1)}, u32[]{:S(2)}) copy-start(bf16[4,32,4096]{2,1,0:T(8,128)(2,1)S(1)} %constant_dynamic-update-slice_fusion) | copy-start | bytes 3145732
  66.7 1.7 copy-start.17
  66.7 1.7 copy-start.21
  83.5 25.5 %copy-start.13 = (pred[4,512]{1,0:T(4,128)(4,1)S(1)}, pred[4,512]{1,0:T(4,128)(4,1)}, u32[]{:S(2)}) copy-start(pred[4,512]{1,0:T(4,128)(4,1)} %iota_compare_fusion.7) | copy-start | bytes 6148
  83.5 25.6 %copy-start.18 = (pred[32]{0:T(512)(128)(4,1)S(1)}, pred[32]{0:T(512)(128)(4,1)}, u32[]{:S(2)}) copy-start(pred[32]{0:T(512)(128)(4,1)} %broadcast_in_dim.247) | copy-start | bytes 100
  83.5 9.2 %collective-permute-start.11 = (f32[4,8,32,4]{1,3,0,2:T(4,128)S(1)}, f32[4,8,32,4]{1,3,0,2:T(4,128)S(1)}, u32[]{:S(2)}, u32[]{:S(2)}) collective-permute-start(f32[4,8,32,4]{1,3,0,2:T(4,128)S(1)} %convolution_bitcast_fusion.4), channel_id=1, source_target_pairs={{0,1},{1,0},{2,3},{3,2},{4,5},{5,4},{6,7},{7,6},{8,9},{9,8},{10,11... | collective-permute-start | bytes 49160 | tf_op jit(solution)/shard_map/ppermute | solution.py:19
  86.1 17.9 %collective-permute-start.10 = (f32[4,8,32,64]{3,1,0,2:T(8,128)S(1)}, f32[4,8,32,64]{3,1,0,2:T(8,128)S(1)}, u32[]{:S(2)}, u32[]{:S(2)}) collective-permute-start(f32[4,8,32,64]{3,1,0,2:T(8,128)S(1)} %convolution_bitcast_fusion.2), channel_id=1, source_target_pairs={{0,1},{1,0},{2,3},{3,2},{4,5},{5,4},{6,7},{7,6},{8,9},{9,8},{10,11... | collective-permute-start | bytes 786440 | tf_op jit(solution)/shard_map/ppermute | solution.py:19
  88.5 20.5 %collective-permute-start.12 = (f32[4,8,4,512]{3,1,0,2:T(8,128)S(1)}, f32[4,8,4,512]{3,1,0,2:T(8,128)S(1)}, u32[]{:S(2)}, u32[]{:S(2)}) collective-permute-start(f32[4,8,4,512]{3,1,0,2:T(8,128)S(1)} %convolution_bitcast_fusion.3), channel_id=1, source_target_pairs={{0,1},{1,0},{2,3},{3,2},{4,5},{5,4},{6,7},{7,6},{8,9},{9,8},{10,11... | collective-permute-start | bytes 786440 | tf_op jit(solution)/shard_map/ppermute | solution.py:19
  92.7 0.7 copy-start.8
  104.0 5.0 %copy-start.6 = (f32[4,8,32,64]{3,1,0,2:T(8,128)}, f32[4,8,32,64]{3,1,0,2:T(8,128)S(1)}, u32[]{:S(2)}) copy-start(f32[4,8,32,64]{3,1,0,2:T(8,128)S(1)} %collective-permute-done.10) | copy-start | bytes 786436
  104.4 21.4 %copy-start.19 = (pred[32]{0:T(512)(128)(4,1)S(1)}, pred[32]{0:T(512)(128)(4,1)}, u32[]{:S(2)}) copy-start(pred[32]{0:T(512)(128)(4,1)} %broadcast_in_dim.247) | copy-start | bytes 100
  112.0 19.2 %copy-start.14 = (pred[4,512]{1,0:T(4,128)(4,1)S(1)}, pred[4,512]{1,0:T(4,128)(4,1)}, u32[]{:S(2)}) copy-start(pred[4,512]{1,0:T(4,128)(4,1)} %iota_compare_fusion.7) | copy-start | bytes 6148
  133.5 1.8 copy-start.9
  133.5 1.8 copy-start.12
  133.5 1.8 copy-start.15
  135.3 1.0 copy-start.4
  135.3 1.2 copy-start.5
  138.1 19.0 %all-to-all-start = ((f32[4,8,32,130]{3,0,2,1:T(4,128)}), f32[4,8,32,130]{3,0,2,1:T(4,128)S(1)}, u32[]{:S(2)}, u32[]{:S(2)}) async-start(f32[4,8,32,130]{3,0,2,1:T(4,128)} %copy.504), calls=%async_computation | async-start | bytes 2097152 | tf_op jit(solution)/shard_map/all_to_all | solution.py:244
  161.1 3.8 %copy-start.20 = (f32[256]{0:T(256)S(1)}, f32[256]{0:T(256)}, u32[]{:S(2)}) copy-start(f32[256]{0:T(256)} %param.20) | copy-start | bytes 3076
  161.8 3.2 %copy-start.2 = (bf16[4,32,4096]{2,1,0:T(8,128)(2,1)S(1)}, bf16[4,32,4096]{2,1,0:T(8,128)(2,1)}, u32[]{:S(2)}) copy-start(bf16[4,32,4096]{2,1,0:T(8,128)(2,1)} %copy-done.1) | copy-start | bytes 3145732
  175.4 3.4 %copy-start.3 = (f32[2,2,2,2,2,4,2048]{6,4,3,2,1,0,5:T(2,128)S(1)}, f32[2,2,2,2,2,4,2048]{6,4,3,2,1,0,5:T(2,128)}, u32[]{:S(2)}) copy-start(f32[2,2,2,2,2,4,2048]{6,4,3,2,1,0,5:T(2,128)} %reshape.509) | copy-start | bytes 3145732
  177.6 8.0 %collective-permute-start.13 = (bf16[2,2,2,2,4,2048]{5,4,2,0,3,1:T(4,128)(2,1)S(1)}, bf16[2,2,2,2,4,2048]{5,4,2,0,3,1:T(4,128)(2,1)}, u32[]{:S(2)}, u32[]{:S(2)}) collective-permute-start(bf16[2,2,2,2,4,2048]{5,4,2,0,3,1:T(4,128)(2,1)S(1)} %bitcast.306), channel_id=1, source_target_pairs={{0,1},{1,0},{2,3},{3,2},{4,5},{5,4},{6,7},{7,6},{8,9},{9,8},{10,11... | collective-permute-start | bytes 786440 | tf_op jit(solution)/shard_map/ppermute | solution.py:19
  181.8 3.8 %copy-start.7 = (f32[2,2,2,2,1,4,2048]{6,4,3,2,1,0,5:T(1,128)S(1)}, f32[2,2,2,2,1,4,2048]{6,4,3,2,1,0,5:T(1,128)}, u32[]{:S(2)}) copy-start(f32[2,2,2,2,1,4,2048]{6,4,3,2,1,0,5:T(1,128)} %constant_dynamic-slice_fusion.3) | copy-start | bytes 1572868
  183.3 9.2 %collective-permute-start.18 = (bf16[2,2,2,2,4,2048]{5,4,1,2,0,3:T(4,128)(2,1)S(1)}, bf16[2,2,2,2,4,2048]{5,4,1,2,0,3:T(4,128)(2,1)S(1)}, u32[]{:S(2)}, u32[]{:S(2)}) collective-permute-start(bf16[2,2,2,2,4,2048]{5,4,1,2,0,3:T(4,128)(2,1)S(1)} %bitcast.307), channel_id=1, source_target_pairs={{0,8},{1,9},{2,10},{3,11},{4,12},{5,13},{6,14},{7,15},{8,0},{9,1},... | collective-permute-start | bytes 786440 | tf_op jit(solution)/shard_map/ppermute | solution.py:19
  187.0 30.4 %copy-start.10 = (bf16[4,1,1,4096]{3,0,2,1:T(4,128)(2,1)S(1)}, bf16[4,1,1,4096]{3,0,2,1:T(4,128)(2,1)}, u32[]{:S(2)}) copy-start(bf16[4,1,1,4096]{3,0,2,1:T(4,128)(2,1)} %param.14) | copy-start | bytes 98308
  187.0 30.4 %copy-start.16 = (f32[4096]{0:T(1024)S(1)}, f32[4096]{0:T(1024)}, u32[]{:S(2)}) copy-start(f32[4096]{0:T(1024)} %param.22) | copy-start | bytes 49156
  187.0 6.9 %collective-permute-start.14 = (bf16[2,2,2,4,2048]{4,3,1,0,2:T(4,128)(2,1)S(1)}, bf16[2,2,2,4,2048]{4,3,1,0,2:T(4,128)(2,1)S(1)}, u32[]{:S(2)}, u32[]{:S(2)}) collective-permute-start(bf16[2,2,2,4,2048]{4,3,1,0,2:T(4,128)(2,1)S(1)} %fusion.49), channel_id=1, source_target_pairs={{0,8},{1,9},{2,10},{3,11},{4,12},{5,13},{6,14},{7,15},{8,0},{9,1},... | collective-permute-start | bytes 393224 | tf_op jit(solution)/shard_map/ppermute | solution.py:19
  193.0 5.3 %collective-permute-start.19 = (bf16[2,2,2,4,2048]{4,3,1,2,0:T(4,128)(2,1)S(1)}, bf16[2,2,2,4,2048]{4,3,1,2,0:T(4,128)(2,1)S(1)}, u32[]{:S(2)}, u32[]{:S(2)}) collective-permute-start(bf16[2,2,2,4,2048]{4,3,1,2,0:T(4,128)(2,1)S(1)} %fusion.50), channel_id=1, source_target_pairs={{0,1},{1,0},{2,3},{3,2},{4,5},{5,4},{6,7},{7,6},{8,9},{9,8},{10,11... | collective-permute-start | bytes 393224 | tf_op jit(solution)/shard_map/ppermute | solution.py:19
  194.1 6.0 %collective-permute-start.15 = (bf16[2,2,4,2048]{3,2,1,0:T(4,128)(2,1)S(1)}, bf16[2,2,4,2048]{3,2,1,0:T(4,128)(2,1)S(1)}, u32[]{:S(2)}, u32[]{:S(2)}) collective-permute-start(bf16[2,2,4,2048]{3,2,1,0:T(4,128)(2,1)S(1)} %fusion.74), channel_id=1, source_target_pairs={{0,2},{1,3},{2,0},{3,1},{4,6},{5,7},{6,4},{7,5},{8,10},{9,11},{10,... | collective-permute-start | bytes 196616 | tf_op jit(solution)/shard_map/ppermute | solution.py:19
  198.4 5.9 %collective-permute-start.20 = (bf16[2,2,4,2048]{3,2,0,1:T(4,128)(2,1)S(1)}, bf16[2,2,4,2048]{3,2,0,1:T(4,128)(2,1)S(1)}, u32[]{:S(2)}, u32[]{:S(2)}) collective-permute-start(bf16[2,2,4,2048]{3,2,0,1:T(4,128)(2,1)S(1)} %fusion.75), channel_id=1, source_target_pairs={{0,16},{1,17},{2,18},{3,19},{4,20},{5,21},{6,22},{7,23},{8,24},{9,... | collective-permute-start | bytes 196616 | tf_op jit(solution)/shard_map/ppermute | solution.py:19
  200.1 5.6 %collective-permute-start.16 = (bf16[2,4,2048]{2,1,0:T(4,128)(2,1)S(1)}, bf16[2,4,2048]{2,1,0:T(4,128)(2,1)S(1)}, u32[]{:S(2)}, u32[]{:S(2)}) collective-permute-start(bf16[2,4,2048]{2,1,0:T(4,128)(2,1)S(1)} %fusion.88), channel_id=1, source_target_pairs={{0,16},{1,17},{2,18},{3,19},{4,20},{5,21},{6,22},{7,23},{8,24},{9,... | collective-permute-start | bytes 98312 | tf_op jit(solution)/shard_map/ppermute | solution.py:19
  204.4 5.3 %collective-permute-start.21 = (bf16[2,4,2048]{2,1,0:T(4,128)(2,1)S(1)}, bf16[2,4,2048]{2,1,0:T(4,128)(2,1)S(1)}, u32[]{:S(2)}, u32[]{:S(2)}) collective-permute-start(bf16[2,4,2048]{2,1,0:T(4,128)(2,1)S(1)} %fusion.89), channel_id=1, source_target_pairs={{0,2},{1,3},{2,0},{3,1},{4,6},{5,7},{6,4},{7,5},{8,10},{9,11},{10,... | collective-permute-start | bytes 98312 | tf_op jit(solution)/shard_map/ppermute | solution.py:19
  205.7 7.7 %collective-permute-start.17 = (bf16[4,2048]{1,0:T(4,128)(2,1)S(1)}, bf16[4,2048]{1,0:T(4,128)(2,1)S(1)}, u32[]{:S(2)}, u32[]{:S(2)}) collective-permute-start(bf16[4,2048]{1,0:T(4,128)(2,1)S(1)} %fusion.93), channel_id=1, source_target_pairs={{0,4},{1,5},{2,6},{3,7},{4,0},{5,1},{6,2},{7,3},{8,12},{9,13},{10,... | collective-permute-start | bytes 49160 | tf_op jit(solution)/shard_map/ppermute | solution.py:19
  209.7 7.7 %collective-permute-start.22 = (bf16[4,2048]{1,0:T(4,128)(2,1)S(1)}, bf16[4,2048]{1,0:T(4,128)(2,1)S(1)}, u32[]{:S(2)}, u32[]{:S(2)}) collective-permute-start(bf16[4,2048]{1,0:T(4,128)(2,1)S(1)} %fusion.94), channel_id=1, source_target_pairs={{0,4},{1,5},{2,6},{3,7},{4,0},{5,1},{6,2},{7,3},{8,12},{9,13},{10,... | collective-permute-start | bytes 49160 | tf_op jit(solution)/shard_map/ppermute | solution.py:19
